TPU v7x, 32 devices: a whole 2x2x4 slice. The times are simulated.
32 devices in a mesh: node: 4 (over x, core), dev: 8 (over z, y).
Axes of the slice: x: 2, y: 2, z: 4, core: 2. Of those that a mesh axis runs over, the one named last changes fastest.
Arguments:
- state: float32 [2, 524288], P(None, ('node', 'dev')), may hold values from -6 to 6
- gates: float32 [4, 2, 128, 128], replicated, may hold values from -0.375 to 0.375
- qubit_order: int32 [14], replicated, may hold values from 0 to 13, each once
Outputs:
- final_state: float32 [2, 524288], P(None, ('node', 'dev'))
Inputs may be any that keep to these rules, and one draw needn't show every extreme that they name: `qubit_order`: a permutation of 0 to 13.
All inputs are finite; a program needn't handle non-finite values.
Results may differ from a plain program's by a relative error of at most 0.00007.
Values sent between devices are 32-bit elements; how exact they have to be, the bound alone decides.
No kernel may reach another device: no remote copies, remote signals or barrier semaphores. Data moves between devices by JAX's collectives and lax.ppermute only.
A program may use at most 64 MiB of HBM per device.

v0:
```python
import jax
import jax.numpy as jnp
from jax import lax
from jax.sharding import PartitionSpec as P


def partner(block, axis, stride):
    count = lax.axis_size(axis)
    route = []
    for low in range(count):
        high = low | 1 << stride
        if high != low and high < count:
            route += [(low, high), (high, low)]
    return lax.ppermute(block, axis, route)


def order_low(planes, qubit_order, gbits):
    low = 2 ** (2 * gbits)
    positions = lax.iota(jnp.int32, low)
    source = jnp.zeros((low,), jnp.int32)
    for j in range(2 * gbits):
        source = source + jnp.left_shift(jnp.right_shift(positions, j) & 1, qubit_order[j])
    blocks = planes.reshape(2, -1, low)
    return jnp.take(blocks, source, axis=2).reshape(2, -1)


def apply_gate(planes, gate, start, gbits):
    width = 2**gbits
    total = planes.shape[1]
    lower = 2**start
    upper = total // (lower * width)
    if lower == 1:
        real_part = planes[0].reshape(upper, width)
        imag_part = planes[1].reshape(upper, width)

        def product(matrix, vector):
            return jnp.einsum("hc,rc->hr", vector, matrix, precision=lax.Precision.HIGHEST)

    else:
        real_part = planes[0].reshape(width, lower)
        imag_part = planes[1].reshape(width, lower)

        def product(matrix, vector):
            return jnp.dot(matrix, vector, precision=lax.Precision.HIGHEST)

    new_real = product(gate[0], real_part) - product(gate[1], imag_part)
    new_imag = product(gate[0], imag_part) + product(gate[1], real_part)
    return jnp.stack([new_real.reshape(-1), new_imag.reshape(-1)])


def local(state, gates, qubit_order):
    gbits = gates.shape[-1].bit_length() - 1
    amps = state.shape[1]
    lbits = amps.bit_length() - 1
    n_node = lax.axis_size("node")
    n_dev = lax.axis_size("dev")
    nbits = n_node.bit_length() - 1
    dbits = n_dev.bit_length() - 1
    planes = order_low(state, qubit_order, gbits)
    planes = apply_gate(planes, gates[0], 0, gbits)
    planes = apply_gate(planes, gates[1], gbits, gbits)
    node_place = lax.axis_index("node")
    for level in range(nbits):
        qubit = lbits - dbits - nbits + level
        lower = 2**qubit
        upper = amps // (2 * lower)
        view = planes.reshape(2, upper, 2, lower)
        lower_half = view[:, :, 0]
        upper_half = view[:, :, 1]
        is_zero = jnp.right_shift(node_place, level) & 1 == 0
        outgoing = jnp.where(is_zero, upper_half, lower_half)
        incoming = partner(outgoing, "node", level)
        new_lower = jnp.where(is_zero, lower_half, incoming)
        new_upper = jnp.where(is_zero, incoming, upper_half)
        planes = jnp.stack([new_lower, new_upper], axis=2).reshape(2, amps)
    blocks = planes.reshape(2, n_dev, amps // n_dev)
    planes = lax.all_to_all(blocks, "dev", split_axis=1, concat_axis=1, tiled=True).reshape(2, amps)
    planes = apply_gate(planes, gates[2], lbits - gbits, gbits)
    planes = apply_gate(planes, gates[3], gbits, gbits)
    return planes


def solution(mesh):
    return jax.shard_map(
        local,
        mesh=mesh,
        in_specs=(P(None, ("node", "dev")), P(), P()),
        out_specs=P(None, ("node", "dev")),
        check_vma=False,
    )
```

profile of v0, /device:TPU:0, one launch (start us, length us, event | category | flops | bytes accessed | tf_op | source)
XLA Modules:
  0.0 129.5 jit_solution(12900502680242877837)
XLA Ops:
  0.0 1.9 %fusion.53 = (s32[1]{0:T(128)}, s32[1]{0:T(128)}, s32[1]{0:T(128)}, s32[1]{0:T(128)}, s32[1]{0:T(128)}, /*index=5*/s32[1]{0:T(128)}, s32[1]{0:T(128)}, s32[1]{0:...) fusion(s32[14]{0:T(128)} %param.5), kind=kLoop, calls=%fused_computation.82 | loop fusion | bytes 112 | tf_op jit(solution)/shard_map/slice | solution.py:22
  1.9 9.7 %compare_select_fusion = s32[16384,1]{0,1:T(1,128)S(1)} fusion(s32[]{:T(128)} %bitcast.13, s32[]{:T(128)} %bitcast.12, s32[]{:T(128)} %bitcast.11, s32[]{:T(128)} %bitcast.10, s32[]{:T(128)} %bitcast.9, s32[]{:T(128)} %bitcast.8, s32[]{:T(128)} %bitcast.7, s32[]{:T(128)} %bitcast.6, s32[]{:T(128)} %bitcast.5, s32[]{:T(128)} %bitcast.4, s32[]{:T(128)} %bitcast.3, ...), kind=kLoop, calls=%fused_computation.16 | loop fusion | flops 950272 | bytes 65592 | tf_op jit(solution)/shard_map/jit(_take)/jit(_where)/select_n | solution.py:24
  11.5 8.8 %compare_and_fusion = pred[16384]{0:T(1024)(128)(4,1)S(1)} fusion(s32[]{:T(128)} %bitcast.13, s32[]{:T(128)} %bitcast.12, s32[]{:T(128)} %bitcast.11, s32[]{:T(128)} %bitcast.10, s32[]{:T(128)} %bitcast.9, s32[]{:T(128)} %bitcast.8, s32[]{:T(128)} %bitcast.7, s32[]{:T(128)} %bitcast.6, s32[]{:T(128)} %bitcast.5, s32[]{:T(128)} %bitcast.4, s32[]{:T(128)} %bitcast.3, ...), kind=kLoop, calls=%fused_computation.59 | loop fusion | flops 999424 | bytes 16440 | tf_op jit(solution)/shard_map/jit(_take)/and | solution.py:24
  20.4 5.5 %copy.14 = f32[2,16384]{0,1:T(8,128)} copy(f32[2,16384]{1,0:T(2,128)} %param.3) | data formatting | bytes 262144 | tf_op args[0]
  26.0 58.2 %gather_fusion = f32[16384,2]{1,0:T(8,128)} fusion(f32[2,16384]{0,1:T(8,128)} %copy.14, s32[16384]{0:T(1024)S(1)} %broadcast_clamp_fusion), kind=kCustom, calls=%fused_computation | custom fusion | bytes 327680 | tf_op jit(solution)/shard_map/jit(_take)/gather | solution.py:24
  84.1 11.8 %bitcast_select_fusion = f32[2,1,16384]{0,2,1:T(8,128)S(1)} fusion(f32[16384,2]{1,0:T(8,128)} %gather_fusion, pred[16384]{0:T(1024)(128)(4,1)S(1)} %compare_and_fusion), kind=kLoop, calls=%fused_computation.3 | loop fusion | flops 32768 | bytes 278528 | tf_op jit(solution)/shard_map/jit(_take)/select_n | solution.py:24
  95.9 6.7 %slice_reduce_fusion = (f32[16384]{0:T(1024)S(1)}, f32[16384]{0:T(1024)S(1)}) fusion(f32[2,1,16384]{0,2,1:T(8,128)S(1)} %bitcast_select_fusion), kind=kLoop, calls=%fused_computation.1 | loop fusion | bytes 262144 | tf_op jit(solution)/shard_map/slice | solution.py:34
  103.2 0.3 convolution_add_fusion.3
  103.4 0.3 fusion.26
  104.0 0.3 fusion.28
  104.3 0.3 fusion.2
  104.7 0.3 fusion.3
  105.3 0.5 collective-permute-start
  105.9 0.9 collective-permute-done
  107.2 2.9 %collective-permute-start.1 = (f32[2,8,1024]{2,1,0:T(8,128)S(1)}, f32[2,8,1024]{2,1,0:T(8,128)S(1)}, u32[]{:S(2)}, u32[]{:S(2)}) collective-permute-start(f32[2,8,1024]{2,1,0:T(8,128)S(1)} %bitcast_select_fusion.2), channel_id=1, source_target_pairs={{0,16},{16,0},{8,24},{24,8},{1,17},{17,1},{9,25},{25,9},{2,18},{18... | collective-permute-start | bytes 196616 | tf_op jit(solution)/shard_map/ppermute | solution.py:14
  110.1 2.4 %collective-permute-done.1 = f32[2,8,1024]{2,1,0:T(8,128)S(1)} collective-permute-done((f32[2,8,1024]{2,1,0:T(8,128)S(1)}, f32[2,8,1024]{2,1,0:T(8,128)S(1)}, u32[]{:S(2)}, u32[]{:S(2)}) %collective-permute-start.1) | collective-permute-done | bytes 65568 | tf_op jit(solution)/shard_map/ppermute | solution.py:14
  112.9 13.3 %all_to_all.5 = f32[2,8,2048]{2,0,1:T(2,128)S(1)} all-to-all(f32[2,8,2048]{2,0,1:T(2,128)S(1)} %reshape.292), channel_id=1, replica_groups=mesh['node'=4,'dev'=8] {'dev'}, dimensions={1} | all-to-all | bytes 262144 | tf_op jit(solution)/shard_map/all_to_all | solution.py:77
  126.3 0.3 fusion.22
  126.6 0.3 fusion.20
  126.9 0.3 convolution_subtract_fusion.1
  127.4 0.3 convolution_add_fusion.1
  128.0 0.3 fusion.1
  128.4 0.3 fusion
  128.8 0.8 pad_maximum_fusion.2
  (29 shorter events, 2.7 us)
Async XLA Ops:
  95.9 6.7 %copy-start = (f32[4,2,128,128]{3,2,1,0:T(8,128)S(1)}, f32[4,2,128,128]{3,2,1,0:T(8,128)}, u32[]{:S(2)}) copy-start(f32[4,2,128,128]{3,2,1,0:T(8,128)} %param.4) | copy-start | bytes 1572868
  105.3 1.4 %collective-permute-start = (f32[2,16,512]{2,1,0:T(8,128)S(1)}, f32[2,16,512]{2,1,0:T(8,128)S(1)}, u32[]{:S(2)}, u32[]{:S(2)}) collective-permute-start(f32[2,16,512]{2,1,0:T(8,128)S(1)} %bitcast_select_fusion.4), channel_id=1, source_target_pairs={{0,8},{8,0},{16,24},{24,16},{1,9},{9,1},{17,25},{25,17},{2,10},{10... | collective-permute-start | bytes 196616 | tf_op jit(solution)/shard_map/ppermute | solution.py:14
  107.2 5.3 %collective-permute-start.1 = (f32[2,8,1024]{2,1,0:T(8,128)S(1)}, f32[2,8,1024]{2,1,0:T(8,128)S(1)}, u32[]{:S(2)}, u32[]{:S(2)}) collective-permute-start(f32[2,8,1024]{2,1,0:T(8,128)S(1)} %bitcast_select_fusion.2), channel_id=1, source_target_pairs={{0,16},{16,0},{8,24},{24,8},{1,17},{17,1},{9,25},{25,9},{2,18},{18... | collective-permute-start | bytes 196616 | tf_op jit(solution)/shard_map/ppermute | solution.py:14
where the time goes:
time: 130 us
  local copies, waits for them, and re-layouts  73.5 us (57%)
  other arithmetic  31.2 us (24%)
  blocking collectives  13.3 us (10%)
  matrix products  4.44 us (3%)
  starting transfers between devices  3.42 us (3%)
  waiting for transfers between devices  3.32 us (3%)
    gather x1, local copies, waits for them, and re-layouts, order_low(): return jnp.take(blocks, source, axis=2).reshape(2, -1)  58.2 us
    select_n x2, other arithmetic, order_low(): return jnp.take(blocks, source, axis=2).reshape(2, -1)  21.5 us
    all_to_all x1, blocking collectives, local(): lax.all_to_all(blocks, 'dev', split_axis=1, concat_axis=1, tiled=True)  13.3 us
    and x1, other arithmetic, order_low(): return jnp.take(blocks, source, axis=2).reshape(2, -1)  8.85 us
    slice x1, local copies, waits for them, and re-layouts, apply_gate(): imag_part = planes[1].reshape(upper, width)  6.7 us
    unnamed x4, local copies, waits for them, and re-layouts  5.56 us
    ppermute x2, starting transfers between devices, partner(): return lax.ppermute(block, axis, route)  3.42 us
    dot_general x12, matrix products, product(): return jnp.dot(matrix, vector, precision=lax.Precision.HIGHEST)  3.36 us
  transfers between devices with their start and end apart: 2, of which 2 were waited for; matrix products, arithmetic and copies ran while one was open for 0% of the time, Pallas kernels for 0%

commit v1 on v0

v1 whole, which is shorter than its diff:
```python
import jax
import jax.numpy as jnp
from jax import lax
from jax.sharding import PartitionSpec as P

HI = lax.Precision.HIGHEST


def mm(a, b):
    return jnp.matmul(a, b, precision=HI)


def layout_maps(qubit_order, gbits):
    width = 2**gbits
    q = qubit_order.astype(jnp.int32)
    j = jnp.arange(2 * gbits)
    crossing = jnp.where(j < gbits, q >= gbits, q < gbits).reshape(2, gbits)
    k = jnp.sum(crossing[0].astype(jnp.int32))
    cross_i = crossing.astype(jnp.int32)
    before_cross = jnp.cumsum(cross_i, axis=1) - cross_i
    before_stay = jnp.cumsum(1 - cross_i, axis=1) - (1 - cross_i)
    pos = jnp.where(crossing, before_cross, k + before_stay).reshape(2 * gbits)
    iota = jnp.arange(width, dtype=jnp.int32)
    bits = jnp.right_shift(iota[None, :], (q % gbits)[:, None]) & 1
    contrib = jnp.left_shift(bits, pos[:, None])
    row_to = jnp.sum(jnp.where(q[:, None] >= gbits, contrib, 0), axis=0)
    col_to = jnp.sum(jnp.where(q[:, None] < gbits, contrib, 0), axis=0)
    own = jnp.right_shift(iota[None, :], jnp.arange(gbits)[:, None]) & 1
    row_from = jnp.sum(jnp.left_shift(own, pos[gbits:, None]), axis=0)
    col_from = jnp.sum(jnp.left_shift(own, pos[:gbits, None]), axis=0)
    f32 = jnp.float32
    a = (iota[:, None] == row_to[None, :]).astype(f32)
    b = (col_to[:, None] == iota[None, :]).astype(f32)
    c = (row_from[:, None] == iota[None, :]).astype(f32)
    d = (iota[:, None] == col_from[None, :]).astype(f32)
    return a, b, c, d, k


def swap_low_bits(planes, k, gbits):
    width = 2**gbits
    rows = lax.broadcasted_iota(jnp.int32, (width, width), 0)
    cols = lax.broadcasted_iota(jnp.int32, (width, width), 1)
    for u in range(gbits):
        hi = 2 ** (gbits - 1 - u)
        lo = 2**u
        view = planes.reshape(2, hi, 2, lo, hi, 2, lo)
        flipped = jnp.flip(view, axis=(2, 5)).reshape(planes.shape)
        differ = (jnp.right_shift(rows, u) & 1) != (jnp.right_shift(cols, u) & 1)
        take = differ & (u < k)
        planes = jnp.where(take[None], flipped, planes)
    return planes


def cmul_left(gr, gi, xr, xi):
    return mm(gr, xr) - mm(gi, xi), mm(gr, xi) + mm(gi, xr)


def cmul_right(xr, xi, hr, hi):
    return mm(xr, hr) - mm(xi, hi), mm(xr, hi) + mm(xi, hr)


def local(state, gates, qubit_order):
    gbits = gates.shape[-1].bit_length() - 1
    width = 2**gbits
    amps = state.shape[1]
    a, b, c, d, k = layout_maps(qubit_order, gbits)
    planes = state.reshape(2, width, width)
    planes = jnp.einsum("xr,prc,cy->pxy", a, planes, b, precision=HI)
    planes = swap_low_bits(planes, k, gbits)
    g0 = gates[0]
    g1 = gates[1]
    h0r = mm(d, g0[0].T)
    h0i = mm(d, g0[1].T)
    g1r = mm(g1[0], c)
    g1i = mm(g1[1], c)
    ur, ui = cmul_right(planes[0], planes[1], h0r, h0i)
    yr, yi = cmul_left(g1r, g1i, ur, ui)
    n_dev = lax.axis_size("dev")
    n_node = lax.axis_size("node")
    blocks = jnp.stack([yr, yi]).reshape(2, n_dev * n_node, -1)
    blocks = lax.all_to_all(blocks, ("dev", "node"), 1, 1, tiled=True)
    w = blocks.reshape(2, width, amps // width)
    g2 = gates[2]
    g3 = gates[3]
    vr, vi = cmul_left(g2[0], g2[1], w[0], w[1])
    zr, zi = cmul_left(g3[0], g3[1], vr, vi)
    return jnp.stack([zr.reshape(-1), zi.reshape(-1)])


def solution(mesh):
    return jax.shard_map(
        local,
        mesh=mesh,
        in_specs=(P(None, ("node", "dev")), P(), P()),
        out_specs=P(None, ("node", "dev")),
        check_vma=False,
    )
```

time: 130 us -> 198 us (1.52)
  local copies, waits for them, and re-layouts: 73.5 us -> 160 us
  other arithmetic: 31.2 us -> 5.47 us
  matrix products: 4.44 us -> 9.95 us
  between operations: 0.28 us -> 5 us
  starting transfers between devices: 3.42 us -> 0 us
  waiting for transfers between devices: 3.32 us -> 0 us
  blocking collectives: 13.3 us -> 15.3 us
    rev x0 -> x7, local copies, waits for them, and re-layouts: none -> 89.6 us  [swap_low_bits(): flipped = jnp.flip(view, axis=(2, 5)).reshape(planes.shape)]
    reshape x0 -> x15, local copies, waits for them, and re-layouts: none -> 70.1 us  [the longest x7 38.2 us: swap_low_bits(): view = planes.reshape(2, hi, 2, lo, hi, 2, lo)]
    gather x1 -> x0, local copies, waits for them, and re-layouts: 58.2 us -> none  [order_low(): return jnp.take(blocks, source, axis=2).reshape(2, -1)]
    select_n x4 -> x9, other arithmetic: 21.5 us -> 2.1 us  [the longest x1 1.32 us: layout_maps(): bits = jnp.right_shift(iota[None, :], (q % gbits)[:, None]) & 1]
    slice x5 -> x1, local copies, waits for them, and re-layouts: 8.86 us -> 0.1 us  [local(): vr, vi = cmul_left(g2[0], g2[1], w[0], w[1])]
    and x1 -> x14, other arithmetic: 8.85 us -> 0.62 us  [the longest x7 0.59 us: swap_low_bits(): take = differ & (u < k)]
    unnamed x4 -> x2, local copies, waits for them, and re-layouts: 5.56 us -> 0.01 us
    dot_general x16 -> x22, matrix products: 4.44 us -> 9.95 us  [the longest x20 8.56 us: mm(): return jnp.matmul(a, b, precision=HI)]
  transfers between devices with their start and end apart: 2 -> 0, of which waited for: 2 -> 0; matrix products, arithmetic and copies ran while one was open for 0% -> 0% of each run, Pallas kernels for 0% -> 0%
where the time goes in v1:
time: 198 us; the launch traced here: 196 us
  local copies, waits for them, and re-layouts  160 us (81%)
  blocking collectives  15.3 us (8%)
  matrix products  9.95 us (5%)
  other arithmetic  5.47 us (3%)
  between operations  5 us (3%)
    rev x7, local copies, waits for them, and re-layouts, swap_low_bits(): flipped = jnp.flip(view, axis=(2, 5)).reshape(planes.shape)  89.6 us
    reshape x7, local copies, waits for them, and re-layouts, swap_low_bits(): view = planes.reshape(2, hi, 2, lo, hi, 2, lo)  38.2 us
    reshape x7, local copies, waits for them, and re-layouts, swap_low_bits(): flipped = jnp.flip(view, axis=(2, 5)).reshape(planes.shape)  31.8 us
    all_to_all x1, blocking collectives, local(): blocks = lax.all_to_all(blocks, ('dev', 'node'), 1, 1, tiled=True)  15.3 us
    dot_general x20, matrix products, mm(): return jnp.matmul(a, b, precision=HI)  8.56 us

profile of v1, /device:TPU:0, one launch (start us, length us, event | category | flops | bytes accessed | tf_op | source)
XLA Modules:
  0.0 195.9 jit_solution(1426159499016189394)
XLA Ops:
  3.4 1.1 fusion.20
  4.5 1.1 fusion.18
  5.5 1.1 fusion.22
  6.7 1.1 fusion.16
  7.8 1.3 and_select_fusion
  9.2 1.1 convolution_bitcast_fusion
  10.6 9.7 %reshape.274 = f32[2,64,2,1,64,2,1]{5,4,2,1,0,6,3:T(8,128)} reshape(f32[2,128,128]{2,1,0:T(8,128)S(1)} %fusion.32) | data formatting | bytes 262144 | tf_op jit(solution)/shard_map/reshape | solution.py:46
  20.4 13.1 %rev.28 = f32[2,64,2,1,64,2,1]{5,4,2,1,0,6,3:T(8,128)} reverse(f32[2,64,2,1,64,2,1]{5,4,2,1,0,6,3:T(8,128)} %reshape.274), dimensions={2,5} | reverse | bytes 262144 | tf_op jit(solution)/shard_map/jit(_flip)/rev | solution.py:47
  33.5 6.9 %reshape.275 = f32[2,128,128]{2,1,0:T(8,128)S(1)} reshape(f32[2,64,2,1,64,2,1]{5,4,2,1,0,6,3:T(8,128)} %rev.28) | data formatting | bytes 262144 | tf_op jit(solution)/shard_map/reshape | solution.py:47
  40.5 14.2 %reshape.276 = f32[2,32,2,2,32,2,2]{6,5,4,3,2,1,0:T(2,128)} reshape(f32[2,128,128]{2,1,0:T(8,128)S(1)} %broadcast_select_fusion) | data formatting | bytes 262144 | tf_op jit(solution)/shard_map/reshape | solution.py:46
  54.7 40.6 %rev.29 = f32[2,32,2,2,32,2,2]{6,5,4,3,2,1,0:T(2,128)} reverse(f32[2,32,2,2,32,2,2]{6,5,4,3,2,1,0:T(2,128)} %reshape.276), dimensions={2,5} | reverse | bytes 262144 | tf_op jit(solution)/shard_map/jit(_flip)/rev | solution.py:47
  95.3 12.4 %reshape.277 = f32[2,128,128]{2,1,0:T(8,128)S(1)} reshape(f32[2,32,2,2,32,2,2]{6,5,4,3,2,1,0:T(2,128)} %rev.29) | data formatting | bytes 262144 | tf_op jit(solution)/shard_map/reshape | solution.py:47
  108.5 7.8 %reshape.278 = f32[2,16,2,4,16,2,4]{6,5,4,3,2,1,0:T(2,128)} reshape(f32[2,128,128]{2,1,0:T(8,128)S(1)} %broadcast_select_fusion.1) | data formatting | bytes 262144 | tf_op jit(solution)/shard_map/reshape | solution.py:46
  116.3 21.0 %rev.30 = f32[2,16,2,4,16,2,4]{6,5,4,3,2,1,0:T(2,128)} reverse(f32[2,16,2,4,16,2,4]{6,5,4,3,2,1,0:T(2,128)} %reshape.278), dimensions={2,5} | reverse | bytes 262144 | tf_op jit(solution)/shard_map/jit(_flip)/rev | solution.py:47
  137.3 7.6 %reshape.279 = f32[2,128,128]{2,1,0:T(8,128)S(1)} reshape(f32[2,16,2,4,16,2,4]{6,5,4,3,2,1,0:T(2,128)} %rev.30) | data formatting | bytes 262144 | tf_op jit(solution)/shard_map/reshape | solution.py:47
  145.7 4.5 %reshape.280 = f32[2,8,2,8,8,2,8]{6,5,4,3,2,1,0:T(2,128)} reshape(f32[2,128,128]{2,1,0:T(8,128)S(1)} %broadcast_select_fusion.2) | data formatting | bytes 262144 | tf_op jit(solution)/shard_map/reshape | solution.py:46
  150.2 10.1 %rev.31 = f32[2,8,2,8,8,2,8]{6,5,4,3,2,1,0:T(2,128)S(1)} reverse(f32[2,8,2,8,8,2,8]{6,5,4,3,2,1,0:T(2,128)} %reshape.280), dimensions={2,5} | reverse | bytes 262144 | tf_op jit(solution)/shard_map/jit(_flip)/rev | solution.py:47
  160.2 3.0 %reshape.281 = f32[2,128,128]{2,1,0:T(8,128)S(1)} reshape(f32[2,8,2,8,8,2,8]{6,5,4,3,2,1,0:T(2,128)S(1)} %rev.31) | data formatting | bytes 262144 | tf_op jit(solution)/shard_map/reshape | solution.py:47
  164.0 1.4 reshape.282
  165.4 2.8 %rev.32 = f32[2,4,2,16,4,2,16]{6,5,4,3,2,1,0:T(2,128)S(1)} reverse(f32[2,4,2,16,4,2,16]{6,5,4,3,2,1,0:T(2,128)S(1)} %reshape.282), dimensions={2,5} | reverse | bytes 262144 | tf_op jit(solution)/shard_map/jit(_flip)/rev | solution.py:47
  168.2 1.3 reshape.283
  170.6 1.4 rev.33
  177.2 15.3 %all_to_all.5 = f32[2,32,512]{2,0,1:T(2,128)S(1)} all-to-all(f32[2,32,512]{2,0,1:T(2,128)S(1)} %pad_maximum_fusion), channel_id=1, replica_groups=mesh['node'=4,'dev'=8] {'dev','node'}, dimensions={1} | all-to-all | bytes 262144 | tf_op jit(solution)/shard_map/all_to_all | solution.py:81
  195.1 0.8 pad_maximum_fusion.1
  (62 shorter events, 10.3 us)
Async XLA Ops:
  160.2 32.4 %copy-start = (f32[4,2,128,128]{3,2,1,0:T(8,128)S(1)}, f32[4,2,128,128]{3,2,1,0:T(8,128)}, u32[]{:S(2)}) copy-start(f32[4,2,128,128]{3,2,1,0:T(8,128)} %param.4) | copy-start | bytes 1572868

commit v2 on v1

v2 whole, which is shorter than its diff:
```python
import jax
import jax.numpy as jnp
from jax import lax
from jax.experimental import pallas as pl
from jax.experimental.pallas import tpu as pltpu
from jax.sharding import PartitionSpec as P

HI = lax.Precision.HIGHEST
F32 = jnp.float32


def mm(a, b):
    return jnp.dot(a, b, precision=HI, preferred_element_type=F32)


def mm_t(a, b):
    return lax.dot_general(a, b, (((1,), (1,)), ((), ())), precision=HI, preferred_element_type=F32)


def flip_bit(x, index, u, axis):
    n = x.shape[axis]
    step = 2**u
    one = pltpu.roll(x, step, axis)
    other = pltpu.roll(x, n - step, axis)
    moved = pltpu.roll(index, step, axis)
    return jnp.where(moved == (index ^ step), one, other)


def first_kernel(q_ref, s_ref, g_ref, y_ref, *, gbits):
    width = 2**gbits
    q = [q_ref[j] for j in range(2 * gbits)]
    is_row_src = [jnp.where(q[j] >= gbits, 1, 0) for j in range(2 * gbits)]
    crossing = [is_row_src[j] if j < gbits else 1 - is_row_src[j] for j in range(2 * gbits)]
    k = sum(crossing[:gbits])
    pos = []
    for group in range(2):
        n_cross = 0
        n_stay = 0
        for t in range(gbits):
            cr = crossing[group * gbits + t]
            pos.append(jnp.where(cr == 1, n_cross, k + n_stay))
            n_cross = n_cross + cr
            n_stay = n_stay + (1 - cr)
    rows = lax.broadcasted_iota(jnp.int32, (width, width), 0)
    cols = lax.broadcasted_iota(jnp.int32, (width, width), 1)
    row_to = jnp.zeros((width, width), jnp.int32)
    col_to = jnp.zeros((width, width), jnp.int32)
    for j in range(2 * gbits):
        bit_at = q[j] - gbits * is_row_src[j]
        row_to = row_to + is_row_src[j] * jnp.left_shift(jnp.right_shift(cols, bit_at) & 1, pos[j])
        col_to = col_to + (1 - is_row_src[j]) * jnp.left_shift(jnp.right_shift(rows, bit_at) & 1, pos[j])
    row_from = jnp.zeros((width, width), jnp.int32)
    col_from = jnp.zeros((width, width), jnp.int32)
    for t in range(gbits):
        row_from = row_from + jnp.left_shift(jnp.right_shift(rows, t) & 1, pos[gbits + t])
        col_from = col_from + jnp.left_shift(jnp.right_shift(cols, t) & 1, pos[t])
    a = (rows == row_to).astype(F32)
    b = (cols == col_to).astype(F32)
    c = (cols == row_from).astype(F32)
    d = (rows == col_from).astype(F32)
    planes = []
    for p in range(2):
        x = mm(mm(a, s_ref[p]), b)
        for u in range(gbits):
            flipped = flip_bit(flip_bit(x, rows, u, 0), cols, u, 1)
            differ = (jnp.right_shift(rows ^ cols, u) & 1) == 1
            x = jnp.where(differ & (u < k), flipped, x)
        planes.append(x)
    xr, xi = planes
    h0r = mm_t(d, g_ref[0, 0])
    h0i = mm_t(d, g_ref[0, 1])
    g1r = mm(g_ref[1, 0], c)
    g1i = mm(g_ref[1, 1], c)
    ur = mm(xr, h0r) - mm(xi, h0i)
    ui = mm(xr, h0i) + mm(xi, h0r)
    y_ref[0] = mm(g1r, ur) - mm(g1i, ui)
    y_ref[1] = mm(g1r, ui) + mm(g1i, ur)


def second_kernel(w_ref, g_ref, z_ref):
    wr = w_ref[0]
    wi = w_ref[1]
    vr = mm(g_ref[0, 0], wr) - mm(g_ref[0, 1], wi)
    vi = mm(g_ref[0, 0], wi) + mm(g_ref[0, 1], wr)
    z_ref[0] = mm(g_ref[1, 0], vr) - mm(g_ref[1, 1], vi)
    z_ref[1] = mm(g_ref[1, 0], vi) + mm(g_ref[1, 1], vr)


def local(state, gates, qubit_order):
    gbits = gates.shape[-1].bit_length() - 1
    width = 2**gbits
    planes = state.reshape(2, width, width)
    y = pl.pallas_call(
        lambda *refs: first_kernel(*refs, gbits=gbits),
        out_shape=jax.ShapeDtypeStruct((2, width, width), F32),
        grid=(1,),
        in_specs=[
            pl.BlockSpec(memory_space=pltpu.SMEM),
            pl.BlockSpec((2, width, width), lambda i: (0, 0, 0)),
            pl.BlockSpec((2, 2, width, width), lambda i: (0, 0, 0, 0)),
        ],
        out_specs=pl.BlockSpec((2, width, width), lambda i: (0, 0, 0)),
    )(qubit_order.astype(jnp.int32), planes, gates)
    parts = lax.axis_size("dev") * lax.axis_size("node")
    if width % parts == 0:
        w = lax.all_to_all(y, ("dev", "node"), 1, 1, tiled=True)
    else:
        w = lax.all_to_all(y.reshape(2, parts, -1), ("dev", "node"), 1, 1, tiled=True)
        w = w.reshape(2, width, width)
    z = pl.pallas_call(
        second_kernel,
        out_shape=jax.ShapeDtypeStruct((2, width, width), F32),
        grid=(1,),
        in_specs=[
            pl.BlockSpec((2, width, width), lambda i: (0, 0, 0)),
            pl.BlockSpec((2, 2, width, width), lambda i: (1, 0, 0, 0)),
        ],
        out_specs=pl.BlockSpec((2, width, width), lambda i: (0, 0, 0)),
    )(w, gates)
    return z.reshape(2, -1)


def solution(mesh):
    return jax.shard_map(
        local,
        mesh=mesh,
        in_specs=(P(None, ("node", "dev")), P(), P()),
        out_specs=P(None, ("node", "dev")),
        check_vma=False,
    )
```

time: 198 us -> 26.5 us (0.13)
  local copies, waits for them, and re-layouts: 160 us -> 4.9 us
  matrix products: 9.95 us -> 0 us
  Pallas kernels: 0 us -> 6 us
  other arithmetic: 5.47 us -> 0 us
  between operations: 5 us -> 0.01 us
    rev x7 -> x0, local copies, waits for them, and re-layouts: 89.6 us -> none  [swap_low_bits(): flipped = jnp.flip(view, axis=(2, 5)).reshape(planes.shape)]
    reshape x15 -> x0, local copies, waits for them, and re-layouts: 70.1 us -> none  [the longest x7 38.2 us: swap_low_bits(): view = planes.reshape(2, hi, 2, lo, hi, 2, lo)]
    dot_general x22 -> x0, matrix products: 9.95 us -> none  [the longest x20 8.56 us: mm(): return jnp.matmul(a, b, precision=HI)]
    pallas_call x0 -> x2, Pallas kernels: none -> 6 us  [the longest x1 3.62 us: local(): pl.pallas_call(lambda *refs: first_kernel(*refs, gbits=gbits), out_shape=...]
    unnamed x2, local copies, waits for them, and re-layouts: 0.01 us -> 3.23 us
    select_n x9 -> x0, other arithmetic: 2.1 us -> none  [the longest x1 1.32 us: layout_maps(): bits = jnp.right_shift(iota[None, :], (q % gbits)[:, None]) & 1]
where the time goes in v2:
time: 26.5 us; the launch traced here: 26.2 us
  blocking collectives  15.3 us (58%)
  Pallas kernels  6 us (23%)
  local copies, waits for them, and re-layouts  4.9 us (18%)
    all_to_all x1, blocking collectives, local(): w = lax.all_to_all(y, ('dev', 'node'), 1, 1, tiled=True)  15.3 us
    pallas_call x1, Pallas kernels, local(): pl.pallas_call(lambda *refs: first_kernel(*refs, gbits=gbits), out_shape=...  3.62 us
    unnamed x2, local copies, waits for them, and re-layouts  3.23 us
    pallas_call x1, Pallas kernels, local(): pl.pallas_call(second_kernel, out_shape=jax.ShapeDtypeStruct((2, width, w...  2.38 us
    pallas_call x1, local copies, waits for them, and re-layouts, local(): pl.pallas_call(lambda *refs: first_kernel(*refs, gbits=gbits), out_shape=...  1.01 us
    all_to_all x1, local copies, waits for them, and re-layouts, local(): w = lax.all_to_all(y, ('dev', 'node'), 1, 1, tiled=True)  0.66 us

profile of v2, /device:TPU:0, one launch (start us, length us, event | category | flops | bytes accessed | tf_op | source)
XLA Modules:
  0.0 26.2 jit_solution(6749519708815938094)
XLA Ops:
  0.0 1.6 %copy.11 = f32[1,2,128,128]{3,2,1,0:T(8,128)} copy(f32[1,2,128,128]{3,1,2,0:T(2,128)} %bitcast.10) | data formatting | bytes 262144
  1.6 3.6 %shard_map.37 = f32[2,128,128]{2,1,0:T(8,128)} custom-call(s32[14]{0:T(128)} %refs_0_.1, f32[2,128,128]{2,1,0:T(8,128)} %bitcast.9, f32[4,2,128,128]{3,2,1,0:T(8,128)} %g_ref.1), custom_call_target="tpu_custom_call" | custom-call | tf_op jit(solution)/shard_map/pallas_call | solution.py:93
  5.2 1.0 %copy.4 = f32[2,128,128]{2,0,1:T(2,128)S(1)} copy(f32[2,128,128]{2,1,0:T(8,128)} %shard_map.37) | data formatting | bytes 262144 | tf_op jit(solution)/shard_map/pallas_call | solution.py:93
  6.2 15.3 %all_to_all.5 = f32[2,128,128]{2,0,1:T(2,128)S(1)} all-to-all(f32[2,128,128]{2,0,1:T(2,128)S(1)} %copy.4), channel_id=1, replica_groups=mesh['node'=4,'dev'=8] {'dev','node'}, dimensions={1} | all-to-all | bytes 262144 | tf_op jit(solution)/shard_map/all_to_all | solution.py:106
  21.5 0.7 %copy.5.w_ref = f32[2,128,128]{2,1,0:T(8,128)} copy(f32[2,128,128]{2,0,1:T(2,128)S(1)} %all_to_all.5) | data formatting | bytes 262144 | tf_op jit(solution)/shard_map/all_to_all | solution.py:106
  22.2 2.4 %shard_map.38 = f32[2,128,128]{2,1,0:T(8,128)} custom-call(f32[2,128,128]{2,1,0:T(8,128)} %copy.5.w_ref, f32[4,2,128,128]{3,2,1,0:T(8,128)} %g_ref.1), custom_call_target="tpu_custom_call" | custom-call | tf_op jit(solution)/shard_map/pallas_call | solution.py:110
  24.6 1.7 %copy.10 = f32[1,2,128,128]{3,1,2,0:T(2,128)} copy(f32[1,2,128,128]{3,2,1,0:T(8,128)} %bitcast.8) | data formatting | bytes 262144

commit v3 on v2

--- a/solution.py
+++ b/solution.py
@@ -60,7 +60,7 @@
     d = (rows == col_from).astype(F32)
     planes = []
     for p in range(2):
-        x = mm(mm(a, s_ref[p]), b)
+        x = mm(mm(a, s_ref[pl.ds(p, width, stride=2), :]), b)
         for u in range(gbits):
             flipped = flip_bit(flip_bit(x, rows, u, 0), cols, u, 1)
             differ = (jnp.right_shift(rows ^ cols, u) & 1) == 1
@@ -73,51 +73,59 @@
     g1i = mm(g_ref[1, 1], c)
     ur = mm(xr, h0r) - mm(xi, h0i)
     ui = mm(xr, h0i) + mm(xi, h0r)
-    y_ref[0] = mm(g1r, ur) - mm(g1i, ui)
-    y_ref[1] = mm(g1r, ui) + mm(g1i, ur)
+    y_ref[pl.ds(0, width, stride=2), :] = mm(g1r, ur) - mm(g1i, ui)
+    y_ref[pl.ds(1, width, stride=2), :] = mm(g1r, ui) + mm(g1i, ur)
 
 
 def second_kernel(w_ref, g_ref, z_ref):
-    wr = w_ref[0]
-    wi = w_ref[1]
+    width = g_ref.shape[-1]
+    wr = w_ref[pl.ds(0, width, stride=2), :]
+    wi = w_ref[pl.ds(1, width, stride=2), :]
     vr = mm(g_ref[0, 0], wr) - mm(g_ref[0, 1], wi)
     vi = mm(g_ref[0, 0], wi) + mm(g_ref[0, 1], wr)
-    z_ref[0] = mm(g_ref[1, 0], vr) - mm(g_ref[1, 1], vi)
-    z_ref[1] = mm(g_ref[1, 0], vi) + mm(g_ref[1, 1], vr)
+    z_ref[pl.ds(0, width, stride=2), :] = mm(g_ref[1, 0], vr) - mm(g_ref[1, 1], vi)
+    z_ref[pl.ds(1, width, stride=2), :] = mm(g_ref[1, 0], vi) + mm(g_ref[1, 1], vr)
+
+
+def exchange(y, width):
+    parts = lax.axis_size("dev") * lax.axis_size("node")
+    axes = ("dev", "node")
+    if width % parts == 0:
+        return lax.all_to_all(y, axes, 0, 0, tiled=True)
+    split = parts // width
+    v = y.reshape(width, 2, split, width // split).transpose(0, 2, 1, 3)
+    v = lax.all_to_all(v.reshape(parts, -1), axes, 0, 0, tiled=True)
+    v = v.reshape(width, split, 2, width // split).transpose(0, 2, 1, 3)
+    return v.reshape(width, 2, width)
 
 
 def local(state, gates, qubit_order):
     gbits = gates.shape[-1].bit_length() - 1
     width = 2**gbits
-    planes = state.reshape(2, width, width)
+    rows = state.reshape(2, width, width).transpose(1, 0, 2).reshape(2 * width, width)
     y = pl.pallas_call(
         lambda *refs: first_kernel(*refs, gbits=gbits),
-        out_shape=jax.ShapeDtypeStruct((2, width, width), F32),
+        out_shape=jax.ShapeDtypeStruct((2 * width, width), F32),
         grid=(1,),
         in_specs=[
             pl.BlockSpec(memory_space=pltpu.SMEM),
-            pl.BlockSpec((2, width, width), lambda i: (0, 0, 0)),
+            pl.BlockSpec((2 * width, width), lambda i: (0, 0)),
             pl.BlockSpec((2, 2, width, width), lambda i: (0, 0, 0, 0)),
         ],
-        out_specs=pl.BlockSpec((2, width, width), lambda i: (0, 0, 0)),
-    )(qubit_order.astype(jnp.int32), planes, gates)
-    parts = lax.axis_size("dev") * lax.axis_size("node")
-    if width % parts == 0:
-        w = lax.all_to_all(y, ("dev", "node"), 1, 1, tiled=True)
-    else:
-        w = lax.all_to_all(y.reshape(2, parts, -1), ("dev", "node"), 1, 1, tiled=True)
-        w = w.reshape(2, width, width)
+        out_specs=pl.BlockSpec((2 * width, width), lambda i: (0, 0)),
+    )(qubit_order.astype(jnp.int32), rows, gates)
+    w = exchange(y.reshape(width, 2, width), width).reshape(2 * width, width)
     z = pl.pallas_call(
         second_kernel,
-        out_shape=jax.ShapeDtypeStruct((2, width, width), F32),
+        out_shape=jax.ShapeDtypeStruct((2 * width, width), F32),
         grid=(1,),
         in_specs=[
-            pl.BlockSpec((2, width, width), lambda i: (0, 0, 0)),
+            pl.BlockSpec((2 * width, width), lambda i: (0, 0)),
             pl.BlockSpec((2, 2, width, width), lambda i: (1, 0, 0, 0)),
         ],
-        out_specs=pl.BlockSpec((2, width, width), lambda i: (0, 0, 0)),
+        out_specs=pl.BlockSpec((2 * width, width), lambda i: (0, 0)),
     )(w, gates)
-    return z.reshape(2, -1)
+    return z.reshape(width, 2, width).transpose(1, 0, 2).reshape(2, -1)
 
 
 def solution(mesh):

time: 26.5 us -> 21.9 us (0.83)
  local copies, waits for them, and re-layouts: 4.9 us -> 0 us
  blocking collectives: 15.3 us -> 15.6 us
    unnamed x2 -> x0, local copies, waits for them, and re-layouts: 3.23 us -> none
    pallas_call x1 -> x0, local copies, waits for them, and re-layouts: 1.01 us -> none  [local(): pl.pallas_call(lambda *refs: first_kernel(*refs, gbits=gbits), out_shape=...]
    all_to_all x1 -> x0, local copies, waits for them, and re-layouts: 0.66 us -> none  [local(): w = lax.all_to_all(y, ('dev', 'node'), 1, 1, tiled=True)]
    all_to_all x1, blocking collectives: 15.3 us -> 15.6 us  [exchange(): return lax.all_to_all(y, axes, 0, 0, tiled=True)]
where the time goes in v3:
time: 21.9 us; the launch traced here: 21.7 us
  blocking collectives  15.6 us (71%)
  Pallas kernels  6.04 us (28%)
    all_to_all x1, blocking collectives, exchange(): return lax.all_to_all(y, axes, 0, 0, tiled=True)  15.6 us
    pallas_call x1, Pallas kernels, local(): pl.pallas_call(lambda *refs: first_kernel(*refs, gbits=gbits), out_shape=...  3.64 us
    pallas_call x1, Pallas kernels, local(): pl.pallas_call(second_kernel, out_shape=jax.ShapeDtypeStruct((2 * width,...  2.4 us

profile of v3, /device:TPU:0, one launch (start us, length us, event | category | flops | bytes accessed | tf_op | source)
XLA Modules:
  0.0 21.7 jit_solution(17385527845739086632)
XLA Ops:
  0.0 3.6 %shard_map.37 = f32[256,128]{1,0:T(8,128)} custom-call(s32[14]{0:T(128)} %refs_0_.1, f32[256,128]{1,0:T(8,128)} %bitcast.14, f32[4,2,128,128]{3,2,1,0:T(8,128)} %g_ref.1), custom_call_target="tpu_custom_call" | custom-call | tf_op jit(solution)/shard_map/pallas_call | solution.py:106
  3.6 15.6 %all_to_all.5 = f32[128,2,128]{2,1,0:T(2,128)} all-to-all(f32[128,2,128]{2,1,0:T(2,128)} %bitcast.13), channel_id=1, replica_groups=mesh['node'=4,'dev'=8] {'dev','node'}, dimensions={0} | all-to-all | bytes 262144 | tf_op jit(solution)/shard_map/all_to_all | solution.py:94
  19.3 2.4 %shard_map.38 = f32[256,128]{1,0:T(8,128)} custom-call(f32[256,128]{1,0:T(8,128)} %bitcast.12, f32[4,2,128,128]{3,2,1,0:T(8,128)} %g_ref.1), custom_call_target="tpu_custom_call" | custom-call | tf_op jit(solution)/shard_map/pallas_call | solution.py:118

commit v4 on v3

--- a/solution.py
+++ b/solution.py
@@ -26,6 +26,12 @@
     return jnp.where(moved == (index ^ step), one, other)
 
 
+def complex_block(gr, gi):
+    return jnp.concatenate(
+        [jnp.concatenate([gr, -gi], axis=1), jnp.concatenate([gi, gr], axis=1)], axis=0
+    )
+
+
 def first_kernel(q_ref, s_ref, g_ref, y_ref, *, gbits):
     width = 2**gbits
     q = [q_ref[j] for j in range(2 * gbits)]
@@ -41,50 +47,52 @@
             pos.append(jnp.where(cr == 1, n_cross, k + n_stay))
             n_cross = n_cross + cr
             n_stay = n_stay + (1 - cr)
+    lane = lax.broadcasted_iota(jnp.int32, (1, width), 1)
+    row_to = jnp.zeros((1, width), jnp.int32)
+    col_to = jnp.zeros((1, width), jnp.int32)
+    for j in range(2 * gbits):
+        bit = jnp.left_shift(jnp.right_shift(lane, q[j] - gbits * is_row_src[j]) & 1, pos[j])
+        row_to = row_to + is_row_src[j] * bit
+        col_to = col_to + (1 - is_row_src[j]) * bit
+    row_from = jnp.zeros((1, width), jnp.int32)
+    col_from = jnp.zeros((1, width), jnp.int32)
+    for t in range(gbits):
+        row_from = row_from + jnp.left_shift(jnp.right_shift(lane, t) & 1, pos[gbits + t])
+        col_from = col_from + jnp.left_shift(jnp.right_shift(lane, t) & 1, pos[t])
     rows = lax.broadcasted_iota(jnp.int32, (width, width), 0)
-    cols = lax.broadcasted_iota(jnp.int32, (width, width), 1)
-    row_to = jnp.zeros((width, width), jnp.int32)
-    col_to = jnp.zeros((width, width), jnp.int32)
-    for j in range(2 * gbits):
-        bit_at = q[j] - gbits * is_row_src[j]
-        row_to = row_to + is_row_src[j] * jnp.left_shift(jnp.right_shift(cols, bit_at) & 1, pos[j])
-        col_to = col_to + (1 - is_row_src[j]) * jnp.left_shift(jnp.right_shift(rows, bit_at) & 1, pos[j])
-    row_from = jnp.zeros((width, width), jnp.int32)
-    col_from = jnp.zeros((width, width), jnp.int32)
-    for t in range(gbits):
-        row_from = row_from + jnp.left_shift(jnp.right_shift(rows, t) & 1, pos[gbits + t])
-        col_from = col_from + jnp.left_shift(jnp.right_shift(cols, t) & 1, pos[t])
     a = (rows == row_to).astype(F32)
-    b = (cols == col_to).astype(F32)
-    c = (cols == row_from).astype(F32)
+    b_t = (rows == col_to).astype(F32)
+    c_t = (rows == row_from).astype(F32)
     d = (rows == col_from).astype(F32)
-    planes = []
-    for p in range(2):
-        x = mm(mm(a, s_ref[pl.ds(p, width, stride=2), :]), b)
-        for u in range(gbits):
-            flipped = flip_bit(flip_bit(x, rows, u, 0), cols, u, 1)
-            differ = (jnp.right_shift(rows ^ cols, u) & 1) == 1
-            x = jnp.where(differ & (u < k), flipped, x)
-        planes.append(x)
-    xr, xi = planes
-    h0r = mm_t(d, g_ref[0, 0])
-    h0i = mm_t(d, g_ref[0, 1])
-    g1r = mm(g_ref[1, 0], c)
-    g1i = mm(g_ref[1, 1], c)
-    ur = mm(xr, h0r) - mm(xi, h0i)
-    ui = mm(xr, h0i) + mm(xi, h0r)
-    y_ref[pl.ds(0, width, stride=2), :] = mm(g1r, ur) - mm(g1i, ui)
-    y_ref[pl.ds(1, width, stride=2), :] = mm(g1r, ui) + mm(g1i, ur)
+    sr = s_ref[pl.ds(0, width, stride=2), :]
+    si = s_ref[pl.ds(1, width, stride=2), :]
+    x = mm(a, jnp.concatenate([sr, si], axis=1))
+    x = mm_t(jnp.concatenate([x[:, :width], x[:, width:]], axis=0), b_t)
+    rows2 = lax.broadcasted_iota(jnp.int32, (2 * width, width), 0)
+    cols2 = lax.broadcasted_iota(jnp.int32, (2 * width, width), 1)
+    for u in range(gbits):
+        flipped = flip_bit(flip_bit(x, rows2, u, 0), cols2, u, 1)
+        differ = (jnp.right_shift(rows2 ^ cols2, u) & 1) == 1
+        x = jnp.where(differ & (u < k), flipped, x)
+    h0 = mm_t(d, jnp.concatenate([g_ref[0, 0], g_ref[0, 1]], axis=0))
+    h0r = h0[:, :width]
+    h0i = h0[:, width:]
+    u_ri = mm(jnp.concatenate([x[:width], x[width:]], axis=1), jnp.concatenate(
+        [jnp.concatenate([h0r, h0i], axis=1), jnp.concatenate([-h0i, h0r], axis=1)], axis=0
+    ))
+    g1 = mm_t(jnp.concatenate([g_ref[1, 0], g_ref[1, 1]], axis=0), c_t)
+    y = mm(complex_block(g1[:width], g1[width:]), jnp.concatenate([u_ri[:, :width], u_ri[:, width:]], axis=0))
+    y_ref[pl.ds(0, width, stride=2), :] = y[:width]
+    y_ref[pl.ds(1, width, stride=2), :] = y[width:]
 
 
 def second_kernel(w_ref, g_ref, z_ref):
     width = g_ref.shape[-1]
-    wr = w_ref[pl.ds(0, width, stride=2), :]
-    wi = w_ref[pl.ds(1, width, stride=2), :]
-    vr = mm(g_ref[0, 0], wr) - mm(g_ref[0, 1], wi)
-    vi = mm(g_ref[0, 0], wi) + mm(g_ref[0, 1], wr)
-    z_ref[pl.ds(0, width, stride=2), :] = mm(g_ref[1, 0], vr) - mm(g_ref[1, 1], vi)
-    z_ref[pl.ds(1, width, stride=2), :] = mm(g_ref[1, 0], vi) + mm(g_ref[1, 1], vr)
+    w = jnp.concatenate([w_ref[pl.ds(0, width, stride=2), :], w_ref[pl.ds(1, width, stride=2), :]], axis=0)
+    v = mm(complex_block(g_ref[0, 0], g_ref[0, 1]), w)
+    z = mm(complex_block(g_ref[1, 0], g_ref[1, 1]), v)
+    z_ref[pl.ds(0, width, stride=2), :] = z[:width]
+    z_ref[pl.ds(1, width, stride=2), :] = z[width:]
 
 
 def exchange(y, width):

time: 21.9 us -> 22.3 us (1.018)
  Pallas kernels: 6.04 us -> 6.47 us
    pallas_call x1, Pallas kernels: 2.4 us -> 2.75 us  [local(): pl.pallas_call(second_kernel, out_shape=jax.ShapeDtypeStruct((2 * width,...]
where the time goes in v4:
time: 22.3 us; the launch traced here: 22.1 us
  blocking collectives  15.6 us (70%)
  Pallas kernels  6.47 us (29%)
    all_to_all x1, blocking collectives, exchange(): return lax.all_to_all(y, axes, 0, 0, tiled=True)  15.6 us
    pallas_call x1, Pallas kernels, local(): pl.pallas_call(lambda *refs: first_kernel(*refs, gbits=gbits), out_shape=...  3.72 us
    pallas_call x1, Pallas kernels, local(): pl.pallas_call(second_kernel, out_shape=jax.ShapeDtypeStruct((2 * width,...  2.75 us

profile of v4, /device:TPU:0, one launch (start us, length us, event | category | flops | bytes accessed | tf_op | source)
XLA Modules:
  0.0 22.1 jit_solution(11199825692305757569)
XLA Ops:
  0.0 3.7 %shard_map.37 = f32[256,128]{1,0:T(8,128)} custom-call(s32[14]{0:T(128)} %refs_0_.1, f32[256,128]{1,0:T(8,128)} %bitcast.14, f32[4,2,128,128]{3,2,1,0:T(8,128)} %g_ref.1), custom_call_target="tpu_custom_call" | custom-call | tf_op jit(solution)/shard_map/pallas_call | solution.py:114
  3.7 15.6 %all_to_all.5 = f32[128,2,128]{2,1,0:T(2,128)} all-to-all(f32[128,2,128]{2,1,0:T(2,128)} %bitcast.13), channel_id=1, replica_groups=mesh['node'=4,'dev'=8] {'dev','node'}, dimensions={0} | all-to-all | bytes 262144 | tf_op jit(solution)/shard_map/all_to_all | solution.py:102
  19.4 2.7 %shard_map.38 = f32[256,128]{1,0:T(8,128)} custom-call(f32[256,128]{1,0:T(8,128)} %bitcast.12, f32[4,2,128,128]{3,2,1,0:T(8,128)} %g_ref.1), custom_call_target="tpu_custom_call" | custom-call | tf_op jit(solution)/shard_map/pallas_call | solution.py:126

commit v5 on v4

--- a/solution.py
+++ b/solution.py
@@ -89,8 +89,8 @@
 def second_kernel(w_ref, g_ref, z_ref):
     width = g_ref.shape[-1]
     w = jnp.concatenate([w_ref[pl.ds(0, width, stride=2), :], w_ref[pl.ds(1, width, stride=2), :]], axis=0)
-    v = mm(complex_block(g_ref[0, 0], g_ref[0, 1]), w)
-    z = mm(complex_block(g_ref[1, 0], g_ref[1, 1]), v)
+    v = mm(complex_block(g_ref[2, 0], g_ref[2, 1]), w)
+    z = mm(complex_block(g_ref[3, 0], g_ref[3, 1]), v)
     z_ref[pl.ds(0, width, stride=2), :] = z[:width]
     z_ref[pl.ds(1, width, stride=2), :] = z[width:]
 
@@ -128,11 +128,11 @@
         out_shape=jax.ShapeDtypeStruct((2 * width, width), F32),
         grid=(1,),
         in_specs=[
-            pl.BlockSpec((2 * width, width), lambda i: (0, 0)),
-            pl.BlockSpec((2, 2, width, width), lambda i: (1, 0, 0, 0)),
+            pl.BlockSpec(memory_space=pltpu.VMEM),
+            pl.BlockSpec(memory_space=pltpu.VMEM),
         ],
         out_specs=pl.BlockSpec((2 * width, width), lambda i: (0, 0)),
-    )(w, gates)
+    )(pltpu.with_memory_space_constraint(w, pltpu.VMEM), pltpu.with_memory_space_constraint(gates, pltpu.VMEM))
     return z.reshape(width, 2, width).transpose(1, 0, 2).reshape(2, -1)
 
 

time: 22.3 us -> 21.2 us (0.951)
  Pallas kernels: 6.47 us -> 5.5 us
    pallas_call x1, Pallas kernels: 2.75 us -> 1.73 us  [local(): pl.pallas_call(second_kernel, out_shape=jax.ShapeDtypeStruct((2 * width,...]
where the time goes in v5:
time: 21.2 us; the launch traced here: 21 us
  blocking collectives  15.5 us (73%)
  Pallas kernels  5.5 us (26%)
    all_to_all x1, blocking collectives, exchange(): return lax.all_to_all(y, axes, 0, 0, tiled=True)  15.5 us
    pallas_call x1, Pallas kernels, local(): pl.pallas_call(lambda *refs: first_kernel(*refs, gbits=gbits), out_shape=...  3.77 us
    pallas_call x1, Pallas kernels, local(): pl.pallas_call(second_kernel, out_shape=jax.ShapeDtypeStruct((2 * width,...  1.73 us

profile of v5, /device:TPU:0, one launch (start us, length us, event | category | flops | bytes accessed | tf_op | source)
XLA Modules:
  0.0 21.0 jit_solution(10522772697974740473)
XLA Ops:
  0.0 0.0 copy-start
  0.0 3.8 %shard_map.37 = f32[256,128]{1,0:T(8,128)} custom-call(s32[14]{0:T(128)} %refs_0_.1, f32[256,128]{1,0:T(8,128)} %bitcast.14, f32[4,2,128,128]{3,2,1,0:T(8,128)} %g_ref.1), custom_call_target="tpu_custom_call" | custom-call | tf_op jit(solution)/shard_map/pallas_call | solution.py:114
  3.8 15.5 %all_to_all.5 = f32[128,2,128]{2,1,0:T(2,128)S(1)} all-to-all(f32[128,2,128]{2,1,0:T(2,128)} %bitcast.13), channel_id=1, replica_groups=mesh['node'=4,'dev'=8] {'dev','node'}, dimensions={0} | all-to-all | bytes 262144 | tf_op jit(solution)/shard_map/all_to_all | solution.py:102
  19.3 0.0 copy-done
  19.3 1.7 %shard_map.38 = f32[256,128]{1,0:T(8,128)} custom-call(f32[256,128]{1,0:T(8,128)S(1)} %bitcast.12, f32[4,2,128,128]{3,2,1,0:T(8,128)S(1)} %copy-done), custom_call_target="tpu_custom_call" | custom-call | tf_op jit(solution)/shard_map/pallas_call | solution.py:126
Async XLA Ops:
  0.0 19.3 %copy-start = (f32[4,2,128,128]{3,2,1,0:T(8,128)S(1)}, f32[4,2,128,128]{3,2,1,0:T(8,128)}, u32[]{:S(2)}) copy-start(f32[4,2,128,128]{3,2,1,0:T(8,128)} %g_ref.1) | copy-start | bytes 1572868

commit v6 on v5

--- a/solution.py
+++ b/solution.py
@@ -113,14 +113,14 @@
     rows = state.reshape(2, width, width).transpose(1, 0, 2).reshape(2 * width, width)
     y = pl.pallas_call(
         lambda *refs: first_kernel(*refs, gbits=gbits),
-        out_shape=jax.ShapeDtypeStruct((2 * width, width), F32),
+        out_shape=pltpu.VMEM((2 * width, width), F32),
         grid=(1,),
         in_specs=[
             pl.BlockSpec(memory_space=pltpu.SMEM),
             pl.BlockSpec((2 * width, width), lambda i: (0, 0)),
             pl.BlockSpec((2, 2, width, width), lambda i: (0, 0, 0, 0)),
         ],
-        out_specs=pl.BlockSpec((2 * width, width), lambda i: (0, 0)),
+        out_specs=pl.BlockSpec(memory_space=pltpu.VMEM),
     )(qubit_order.astype(jnp.int32), rows, gates)
     w = exchange(y.reshape(width, 2, width), width).reshape(2 * width, width)
     z = pl.pallas_call(

time: 21.2 us -> 20.3 us (0.958)
  Pallas kernels: 5.5 us -> 4.84 us
    pallas_call x1, Pallas kernels: 3.77 us -> 3.11 us  [local(): pl.pallas_call(lambda *refs: first_kernel(*refs, gbits=gbits), out_shape=...]
where the time goes in v6:
time: 20.3 us; the launch traced here: 20.2 us
  blocking collectives  15.3 us (75%)
  Pallas kernels  4.84 us (24%)
    all_to_all x1, blocking collectives, exchange(): return lax.all_to_all(y, axes, 0, 0, tiled=True)  15.3 us
    pallas_call x1, Pallas kernels, local(): pl.pallas_call(lambda *refs: first_kernel(*refs, gbits=gbits), out_shape=...  3.11 us
    pallas_call x1, Pallas kernels, local(): pl.pallas_call(second_kernel, out_shape=jax.ShapeDtypeStruct((2 * width,...  1.73 us

profile of v6, /device:TPU:0, one launch (start us, length us, event | category | flops | bytes accessed | tf_op | source)
XLA Modules:
  0.0 20.2 jit_solution(10997320668004225005)
XLA Ops:
  0.0 0.0 copy-start
  0.0 3.1 %shard_map.37 = f32[256,128]{1,0:T(8,128)S(1)} custom-call(s32[14]{0:T(128)} %refs_0_.1, f32[256,128]{1,0:T(8,128)} %bitcast.14, f32[4,2,128,128]{3,2,1,0:T(8,128)} %g_ref.1), custom_call_target="tpu_custom_call" | custom-call | tf_op jit(solution)/shard_map/pallas_call | solution.py:114
  3.1 15.3 %all_to_all.5 = f32[128,2,128]{2,1,0:T(2,128)S(1)} all-to-all(f32[128,2,128]{2,1,0:T(2,128)S(1)} %bitcast.13), channel_id=1, replica_groups=mesh['node'=4,'dev'=8] {'dev','node'}, dimensions={0} | all-to-all | bytes 262144 | tf_op jit(solution)/shard_map/all_to_all | solution.py:102
  18.5 0.0 copy-done
  18.5 1.7 %shard_map.38 = f32[256,128]{1,0:T(8,128)} custom-call(f32[256,128]{1,0:T(8,128)S(1)} %bitcast.12, f32[4,2,128,128]{3,2,1,0:T(8,128)S(1)} %copy-done), custom_call_target="tpu_custom_call" | custom-call | tf_op jit(solution)/shard_map/pallas_call | solution.py:126
Async XLA Ops:
  0.0 18.5 %copy-start = (f32[4,2,128,128]{3,2,1,0:T(8,128)S(1)}, f32[4,2,128,128]{3,2,1,0:T(8,128)}, u32[]{:S(2)}) copy-start(f32[4,2,128,128]{3,2,1,0:T(8,128)} %g_ref.1) | copy-start | bytes 1572868

commit v7 on v6

--- a/solution.py
+++ b/solution.py
@@ -32,48 +32,68 @@
     )
 
 
-def first_kernel(q_ref, s_ref, g_ref, y_ref, *, gbits):
+def first_kernel(q_ref, s_ref, g_ref, y_ref, x_ref, pair_ref, *, gbits):
     width = 2**gbits
     q = [q_ref[j] for j in range(2 * gbits)]
-    is_row_src = [jnp.where(q[j] >= gbits, 1, 0) for j in range(2 * gbits)]
-    crossing = [is_row_src[j] if j < gbits else 1 - is_row_src[j] for j in range(2 * gbits)]
-    k = sum(crossing[:gbits])
+    for slot in range(2 * (gbits + 1)):
+        pair_ref[slot] = gbits
+    rank_col = 0
+    rank_row = 0
+    for t in range(gbits):
+        col_cross = q[t] >= gbits
+        row_cross = q[gbits + t] < gbits
+        pair_ref[jnp.where(col_cross, rank_col, gbits)] = q[t] - gbits
+        pair_ref[gbits + 1 + jnp.where(row_cross, rank_row, gbits)] = q[gbits + t]
+        rank_col = rank_col + jnp.where(col_cross, 1, 0)
+        rank_row = rank_row + jnp.where(row_cross, 1, 0)
+    row_of = [pair_ref[i] for i in range(gbits)]
+    col_of = [pair_ref[gbits + 1 + i] for i in range(gbits)]
+    partner = [gbits] * gbits
+    partner_back = [gbits] * gbits
+    for i in range(gbits):
+        for a in range(gbits):
+            partner[a] = jnp.where(row_of[i] == a, col_of[i], partner[a])
+            partner_back[a] = jnp.where(col_of[i] == a, row_of[i], partner_back[a])
     pos = []
-    for group in range(2):
-        n_cross = 0
-        n_stay = 0
-        for t in range(gbits):
-            cr = crossing[group * gbits + t]
-            pos.append(jnp.where(cr == 1, n_cross, k + n_stay))
-            n_cross = n_cross + cr
-            n_stay = n_stay + (1 - cr)
+    for j in range(2 * gbits):
+        src = q[j] - gbits if j < gbits else q[j]
+        moved = src
+        for a in range(gbits):
+            moved = jnp.where(src == a, partner[a] if j < gbits else partner_back[a], moved)
+        if j < gbits:
+            pos.append(jnp.where(q[j] >= gbits, moved, q[j]))
+        else:
+            pos.append(jnp.where(q[j] < gbits, moved, q[j] - gbits))
     lane = lax.broadcasted_iota(jnp.int32, (1, width), 1)
-    row_to = jnp.zeros((1, width), jnp.int32)
-    col_to = jnp.zeros((1, width), jnp.int32)
-    for j in range(2 * gbits):
-        bit = jnp.left_shift(jnp.right_shift(lane, q[j] - gbits * is_row_src[j]) & 1, pos[j])
-        row_to = row_to + is_row_src[j] * bit
-        col_to = col_to + (1 - is_row_src[j]) * bit
     row_from = jnp.zeros((1, width), jnp.int32)
     col_from = jnp.zeros((1, width), jnp.int32)
     for t in range(gbits):
         row_from = row_from + jnp.left_shift(jnp.right_shift(lane, t) & 1, pos[gbits + t])
         col_from = col_from + jnp.left_shift(jnp.right_shift(lane, t) & 1, pos[t])
     rows = lax.broadcasted_iota(jnp.int32, (width, width), 0)
-    a = (rows == row_to).astype(F32)
-    b_t = (rows == col_to).astype(F32)
     c_t = (rows == row_from).astype(F32)
     d = (rows == col_from).astype(F32)
-    sr = s_ref[pl.ds(0, width, stride=2), :]
-    si = s_ref[pl.ds(1, width, stride=2), :]
-    x = mm(a, jnp.concatenate([sr, si], axis=1))
-    x = mm_t(jnp.concatenate([x[:, :width], x[:, width:]], axis=0), b_t)
-    rows2 = lax.broadcasted_iota(jnp.int32, (2 * width, width), 0)
-    cols2 = lax.broadcasted_iota(jnp.int32, (2 * width, width), 1)
-    for u in range(gbits):
-        flipped = flip_bit(flip_bit(x, rows2, u, 0), cols2, u, 1)
-        differ = (jnp.right_shift(rows2 ^ cols2, u) & 1) == 1
-        x = jnp.where(differ & (u < k), flipped, x)
+    x_ref[...] = jnp.concatenate(
+        [s_ref[pl.ds(0, width, stride=2), :], s_ref[pl.ds(1, width, stride=2), :]], axis=0
+    )
+    for a in range(gbits):
+        b = partner[a]
+
+        @pl.when(b < gbits)
+        def _():
+            rows2 = lax.broadcasted_iota(jnp.int32, (2 * width, width), 0)
+            cols2 = lax.broadcasted_iota(jnp.int32, (2 * width, width), 1)
+            held = x_ref[...]
+            step = jnp.left_shift(1, b)
+            one = pltpu.roll(held, step, 1)
+            other = pltpu.roll(held, width - step, 1)
+            turned = pltpu.roll(cols2, step, 1)
+            flipped = jnp.where(turned == (cols2 ^ step), one, other)
+            flipped = flip_bit(flipped, rows2, a, 0)
+            differ = ((jnp.right_shift(rows2, a) ^ jnp.right_shift(cols2, b)) & 1) == 1
+            x_ref[...] = jnp.where(differ, flipped, held)
+
+    x = x_ref[...]
     h0 = mm_t(d, jnp.concatenate([g_ref[0, 0], g_ref[0, 1]], axis=0))
     h0r = h0[:, :width]
     h0i = h0[:, width:]
@@ -121,6 +141,7 @@
             pl.BlockSpec((2, 2, width, width), lambda i: (0, 0, 0, 0)),
         ],
         out_specs=pl.BlockSpec(memory_space=pltpu.VMEM),
+        scratch_shapes=[pltpu.VMEM((2 * width, width), F32), pltpu.SMEM((2 * (gbits + 1),), jnp.int32)],
     )(qubit_order.astype(jnp.int32), rows, gates)
     w = exchange(y.reshape(width, 2, width), width).reshape(2 * width, width)
     z = pl.pallas_call(

time: 20.3 us -> 20.2 us (level)
  no operation moved by 1% of the time
where the time goes in v7:
time: 20.2 us; the launch traced here: 20.1 us
  blocking collectives  15.3 us (76%)
  Pallas kernels  4.71 us (23%)
    all_to_all x1, blocking collectives, exchange(): return lax.all_to_all(y, axes, 0, 0, tiled=True)  15.3 us
    pallas_call x1, Pallas kernels, local(): pl.pallas_call(lambda *refs: first_kernel(*refs, gbits=gbits), out_shape=...  2.99 us
    pallas_call x1, Pallas kernels, local(): pl.pallas_call(second_kernel, out_shape=jax.ShapeDtypeStruct((2 * width,...  1.73 us

profile of v7, /device:TPU:0, one launch (start us, length us, event | category | flops | bytes accessed | tf_op | source)
XLA Modules:
  0.0 20.1 jit_solution(9080852174515519696)
XLA Ops:
  0.0 0.0 copy-start
  0.0 3.0 %shard_map.37 = f32[256,128]{1,0:T(8,128)S(1)} custom-call(s32[14]{0:T(128)} %refs_0_.1, f32[256,128]{1,0:T(8,128)} %bitcast.14, f32[4,2,128,128]{3,2,1,0:T(8,128)} %g_ref.1), custom_call_target="tpu_custom_call" | custom-call | tf_op jit(solution)/shard_map/pallas_call | solution.py:134
  3.0 15.3 %all_to_all.5 = f32[128,2,128]{2,1,0:T(2,128)S(1)} all-to-all(f32[128,2,128]{2,1,0:T(2,128)S(1)} %bitcast.13), channel_id=1, replica_groups=mesh['node'=4,'dev'=8] {'dev','node'}, dimensions={0} | all-to-all | bytes 262144 | tf_op jit(solution)/shard_map/all_to_all | solution.py:122
  18.3 0.0 copy-done
  18.3 1.7 %shard_map.38 = f32[256,128]{1,0:T(8,128)} custom-call(f32[256,128]{1,0:T(8,128)S(1)} %bitcast.12, f32[4,2,128,128]{3,2,1,0:T(8,128)S(1)} %copy-done), custom_call_target="tpu_custom_call" | custom-call | tf_op jit(solution)/shard_map/pallas_call | solution.py:147
Async XLA Ops:
  0.0 18.3 %copy-start = (f32[4,2,128,128]{3,2,1,0:T(8,128)S(1)}, f32[4,2,128,128]{3,2,1,0:T(8,128)}, u32[]{:S(2)}) copy-start(f32[4,2,128,128]{3,2,1,0:T(8,128)} %g_ref.1) | copy-start | bytes 1572868

commit v8 on v7

--- a/solution.py
+++ b/solution.py
@@ -54,45 +54,56 @@
         for a in range(gbits):
             partner[a] = jnp.where(row_of[i] == a, col_of[i], partner[a])
             partner_back[a] = jnp.where(col_of[i] == a, row_of[i], partner_back[a])
+    row_cross = [partner[u] < gbits for u in range(gbits)]
+    col_cross = [partner_back[u] < gbits for u in range(gbits)]
+    held_at = 0
+    for u in range(gbits):
+        pair_ref[jnp.where(row_cross[u], gbits, held_at)] = u
+        held_at = held_at + jnp.where(row_cross[u], 0, 1)
+    kept = [pair_ref[u] for u in range(gbits)]
+    col_pos = []
+    stay_rank = 0
+    for u in range(gbits):
+        free = kept[0]
+        for r in range(1, gbits):
+            free = jnp.where(stay_rank == r, kept[r], free)
+        col_pos.append(jnp.where(col_cross[u], partner_back[u], free))
+        stay_rank = stay_rank + jnp.where(col_cross[u], 0, 1)
     pos = []
     for j in range(2 * gbits):
-        src = q[j] - gbits if j < gbits else q[j]
-        moved = src
-        for a in range(gbits):
-            moved = jnp.where(src == a, partner[a] if j < gbits else partner_back[a], moved)
         if j < gbits:
-            pos.append(jnp.where(q[j] >= gbits, moved, q[j]))
+            src_col = col_pos[0]
+            for u in range(1, gbits):
+                src_col = jnp.where(q[j] == u, col_pos[u], src_col)
+            pos.append(jnp.where(q[j] >= gbits, q[j] - gbits, src_col))
         else:
-            pos.append(jnp.where(q[j] < gbits, moved, q[j] - gbits))
+            back = partner_back[0]
+            for u in range(1, gbits):
+                back = jnp.where(q[j] == u, partner_back[u], back)
+            pos.append(jnp.where(q[j] < gbits, back, q[j] - gbits))
     lane = lax.broadcasted_iota(jnp.int32, (1, width), 1)
+    col_to = jnp.zeros((1, width), jnp.int32)
     row_from = jnp.zeros((1, width), jnp.int32)
     col_from = jnp.zeros((1, width), jnp.int32)
     for t in range(gbits):
+        col_to = col_to + jnp.left_shift(jnp.right_shift(lane, t) & 1, col_pos[t])
         row_from = row_from + jnp.left_shift(jnp.right_shift(lane, t) & 1, pos[gbits + t])
         col_from = col_from + jnp.left_shift(jnp.right_shift(lane, t) & 1, pos[t])
     rows = lax.broadcasted_iota(jnp.int32, (width, width), 0)
+    b_t = (rows == col_to).astype(F32)
     c_t = (rows == row_from).astype(F32)
     d = (rows == col_from).astype(F32)
-    x_ref[...] = jnp.concatenate(
+    x = jnp.concatenate(
         [s_ref[pl.ds(0, width, stride=2), :], s_ref[pl.ds(1, width, stride=2), :]], axis=0
     )
-    for a in range(gbits):
-        b = partner[a]
-
-        @pl.when(b < gbits)
-        def _():
-            rows2 = lax.broadcasted_iota(jnp.int32, (2 * width, width), 0)
-            cols2 = lax.broadcasted_iota(jnp.int32, (2 * width, width), 1)
-            held = x_ref[...]
-            step = jnp.left_shift(1, b)
-            one = pltpu.roll(held, step, 1)
-            other = pltpu.roll(held, width - step, 1)
-            turned = pltpu.roll(cols2, step, 1)
-            flipped = jnp.where(turned == (cols2 ^ step), one, other)
-            flipped = flip_bit(flipped, rows2, a, 0)
-            differ = ((jnp.right_shift(rows2, a) ^ jnp.right_shift(cols2, b)) & 1) == 1
-            x_ref[...] = jnp.where(differ, flipped, held)
-
+    x = mm_t(x, b_t)
+    rows2 = lax.broadcasted_iota(jnp.int32, (2 * width, width), 0)
+    cols2 = lax.broadcasted_iota(jnp.int32, (2 * width, width), 1)
+    for u in range(gbits):
+        flipped = flip_bit(flip_bit(x, rows2, u, 0), cols2, u, 1)
+        differ = (jnp.right_shift(rows2 ^ cols2, u) & 1) == 1
+        x = jnp.where(differ & row_cross[u], flipped, x)
+    x_ref[...] = x
     x = x_ref[...]
     h0 = mm_t(d, jnp.concatenate([g_ref[0, 0], g_ref[0, 1]], axis=0))
     h0r = h0[:, :width]

time: 20.2 us -> 20.1 us (level)
  no operation moved by 1% of the time
where the time goes in v8:
time: 20.1 us; the launch traced here: 20 us
  blocking collectives  15.3 us (76%)
  Pallas kernels  4.61 us (23%)
    all_to_all x1, blocking collectives, exchange(): return lax.all_to_all(y, axes, 0, 0, tiled=True)  15.3 us
    pallas_call x1, Pallas kernels, local(): pl.pallas_call(lambda *refs: first_kernel(*refs, gbits=gbits), out_shape=...  2.88 us
    pallas_call x1, Pallas kernels, local(): pl.pallas_call(second_kernel, out_shape=jax.ShapeDtypeStruct((2 * width,...  1.73 us

profile of v8, /device:TPU:0, one launch (start us, length us, event | category | flops | bytes accessed | tf_op | source)
XLA Modules:
  0.0 20.0 jit_solution(8662790063003279605)
XLA Ops:
  0.0 0.0 copy-start
  0.0 2.9 %shard_map.37 = f32[256,128]{1,0:T(8,128)S(1)} custom-call(s32[14]{0:T(128)} %refs_0_.1, f32[256,128]{1,0:T(8,128)} %bitcast.14, f32[4,2,128,128]{3,2,1,0:T(8,128)} %g_ref.1), custom_call_target="tpu_custom_call" | custom-call | tf_op jit(solution)/shard_map/pallas_call | solution.py:145
  2.9 15.3 %all_to_all.5 = f32[128,2,128]{2,1,0:T(2,128)S(1)} all-to-all(f32[128,2,128]{2,1,0:T(2,128)S(1)} %bitcast.13), channel_id=1, replica_groups=mesh['node'=4,'dev'=8] {'dev','node'}, dimensions={0} | all-to-all | bytes 262144 | tf_op jit(solution)/shard_map/all_to_all | solution.py:133
  18.2 0.0 copy-done
  18.2 1.7 %shard_map.38 = f32[256,128]{1,0:T(8,128)} custom-call(f32[256,128]{1,0:T(8,128)S(1)} %bitcast.12, f32[4,2,128,128]{3,2,1,0:T(8,128)S(1)} %copy-done), custom_call_target="tpu_custom_call" | custom-call | tf_op jit(solution)/shard_map/pallas_call | solution.py:158
Async XLA Ops:
  0.0 18.2 %copy-start = (f32[4,2,128,128]{3,2,1,0:T(8,128)S(1)}, f32[4,2,128,128]{3,2,1,0:T(8,128)}, u32[]{:S(2)}) copy-start(f32[4,2,128,128]{3,2,1,0:T(8,128)} %g_ref.1) | copy-start | bytes 1572868

commit v9 on v8

--- a/solution.py
+++ b/solution.py
@@ -32,7 +32,7 @@
     )
 
 
-def first_kernel(q_ref, s_ref, g_ref, y_ref, x_ref, pair_ref, *, gbits):
+def first_kernel(q_ref, s_ref, g_ref, h_ref, y_ref, m_ref, x_ref, pair_ref, *, gbits, order):
     width = 2**gbits
     q = [q_ref[j] for j in range(2 * gbits)]
     for slot in range(2 * (gbits + 1)):
@@ -111,26 +111,45 @@
     u_ri = mm(jnp.concatenate([x[:width], x[width:]], axis=1), jnp.concatenate(
         [jnp.concatenate([h0r, h0i], axis=1), jnp.concatenate([-h0i, h0r], axis=1)], axis=0
     ))
-    g1 = mm_t(jnp.concatenate([g_ref[1, 0], g_ref[1, 1]], axis=0), c_t)
+    g1_rows = []
+    for p in range(2):
+        g1_rows += [g_ref[1, p, pl.ds(start, size), :] for start, size in order]
+    g1 = mm_t(jnp.concatenate(g1_rows, axis=0), c_t)
+    cols = lax.broadcasted_iota(jnp.int32, (width, width), 1)
+    taken = jnp.zeros((width, width), jnp.int32)
+    at = 0
+    for start, size in order:
+        inside = (cols >= at) & (cols < at + size)
+        taken = jnp.where(inside, cols - at + start, taken)
+        at += size
+    arrive = (rows == taken).astype(F32)
+    g2 = mm(jnp.concatenate([h_ref[0, 0], h_ref[0, 1]], axis=0), arrive)
+    m_ref[...] = mm(complex_block(h_ref[1, 0], h_ref[1, 1]), g2)
     y = mm(complex_block(g1[:width], g1[width:]), jnp.concatenate([u_ri[:, :width], u_ri[:, width:]], axis=0))
     y_ref[pl.ds(0, width, stride=2), :] = y[:width]
     y_ref[pl.ds(1, width, stride=2), :] = y[width:]
 
 
-def second_kernel(w_ref, g_ref, z_ref):
-    width = g_ref.shape[-1]
+def second_kernel(w_ref, m_ref, z_ref):
+    width = m_ref.shape[-1]
     w = jnp.concatenate([w_ref[pl.ds(0, width, stride=2), :], w_ref[pl.ds(1, width, stride=2), :]], axis=0)
-    v = mm(complex_block(g_ref[2, 0], g_ref[2, 1]), w)
-    z = mm(complex_block(g_ref[3, 0], g_ref[3, 1]), v)
+    z = mm(complex_block(m_ref[:width], m_ref[width:]), w)
     z_ref[pl.ds(0, width, stride=2), :] = z[:width]
     z_ref[pl.ds(1, width, stride=2), :] = z[width:]
 
 
+def send_order(width):
+    n_node = lax.axis_size("node")
+    n_dev = lax.axis_size("dev")
+    size = width // (n_node * n_dev)
+    return tuple(((m // n_dev + n_node * (m % n_dev)) * size, size) for m in range(n_node * n_dev))
+
+
 def exchange(y, width):
     parts = lax.axis_size("dev") * lax.axis_size("node")
+    if width % parts == 0:
+        return lax.all_to_all(y, ("node", "dev"), 0, 0, tiled=True)
     axes = ("dev", "node")
-    if width % parts == 0:
-        return lax.all_to_all(y, axes, 0, 0, tiled=True)
     split = parts // width
     v = y.reshape(width, 2, split, width // split).transpose(0, 2, 1, 3)
     v = lax.all_to_all(v.reshape(parts, -1), axes, 0, 0, tiled=True)
@@ -141,30 +160,33 @@
 def local(state, gates, qubit_order):
     gbits = gates.shape[-1].bit_length() - 1
     width = 2**gbits
+    parts = lax.axis_size("dev") * lax.axis_size("node")
+    if width % parts == 0:
+        order = send_order(width)
+    else:
+        order = ((0, width),)
     rows = state.reshape(2, width, width).transpose(1, 0, 2).reshape(2 * width, width)
-    y = pl.pallas_call(
-        lambda *refs: first_kernel(*refs, gbits=gbits),
-        out_shape=pltpu.VMEM((2 * width, width), F32),
+    vmem = pl.BlockSpec(memory_space=pltpu.VMEM)
+    y, m = pl.pallas_call(
+        lambda *refs: first_kernel(*refs, gbits=gbits, order=order),
+        out_shape=(pltpu.VMEM((2 * width, width), F32), pltpu.VMEM((2 * width, width), F32)),
         grid=(1,),
         in_specs=[
             pl.BlockSpec(memory_space=pltpu.SMEM),
             pl.BlockSpec((2 * width, width), lambda i: (0, 0)),
             pl.BlockSpec((2, 2, width, width), lambda i: (0, 0, 0, 0)),
+            pl.BlockSpec((2, 2, width, width), lambda i: (1, 0, 0, 0)),
         ],
-        out_specs=pl.BlockSpec(memory_space=pltpu.VMEM),
+        out_specs=(vmem, vmem),
         scratch_shapes=[pltpu.VMEM((2 * width, width), F32), pltpu.SMEM((2 * (gbits + 1),), jnp.int32)],
-    )(qubit_order.astype(jnp.int32), rows, gates)
+    )(qubit_order.astype(jnp.int32), rows, gates, gates)
     w = exchange(y.reshape(width, 2, width), width).reshape(2 * width, width)
     z = pl.pallas_call(
         second_kernel,
         out_shape=jax.ShapeDtypeStruct((2 * width, width), F32),
-        grid=(1,),
-        in_specs=[
-            pl.BlockSpec(memory_space=pltpu.VMEM),
-            pl.BlockSpec(memory_space=pltpu.VMEM),
-        ],
-        out_specs=pl.BlockSpec((2 * width, width), lambda i: (0, 0)),
-    )(pltpu.with_memory_space_constraint(w, pltpu.VMEM), pltpu.with_memory_space_constraint(gates, pltpu.VMEM))
+        in_specs=[vmem, vmem],
+        out_specs=pl.BlockSpec(memory_space=pltpu.VMEM),
+    )(pltpu.with_memory_space_constraint(w, pltpu.VMEM), pltpu.with_memory_space_constraint(m, pltpu.VMEM))
     return z.reshape(width, 2, width).transpose(1, 0, 2).reshape(2, -1)
 
 

time: 20.1 us -> 19.3 us (0.960)
  blocking collectives: 15.3 us -> 14.8 us
  Pallas kernels: 4.61 us -> 4.33 us
    pallas_call x1, Pallas kernels: 1.73 us -> 1.03 us  [local(): pl.pallas_call(second_kernel, out_shape=jax.ShapeDtypeStruct((2 * width,...]
    all_to_all x1, blocking collectives: 15.3 us -> 14.8 us  [exchange(): return lax.all_to_all(y, ('node', 'dev'), 0, 0, tiled=True)]
    pallas_call x1, Pallas kernels: 2.88 us -> 3.3 us  [local(): pl.pallas_call(lambda *refs: first_kernel(*refs, gbits=gbits, order=order...]
where the time goes in v9:
time: 19.3 us; the launch traced here: 19.2 us
  blocking collectives  14.8 us (77%)
  Pallas kernels  4.33 us (22%)
    all_to_all x1, blocking collectives, exchange(): return lax.all_to_all(y, ('node', 'dev'), 0, 0, tiled=True)  14.8 us
    pallas_call x1, Pallas kernels, local(): pl.pallas_call(lambda *refs: first_kernel(*refs, gbits=gbits, order=order...  3.3 us
    pallas_call x1, Pallas kernels, local(): pl.pallas_call(second_kernel, out_shape=jax.ShapeDtypeStruct((2 * width,...  1.03 us

profile of v9, /device:TPU:0, one launch (start us, length us, event | category | flops | bytes accessed | tf_op | source)
XLA Modules:
  0.0 19.2 jit_solution(12076675803073025044)
XLA Ops:
  0.0 3.3 %shard_map.37 = (f32[256,128]{1,0:T(8,128)S(1)}, f32[256,128]{1,0:T(8,128)S(1)}) custom-call(s32[14]{0:T(128)} %refs_0_.1, f32[256,128]{1,0:T(8,128)} %bitcast.14, f32[4,2,128,128]{3,2,1,0:T(8,128)} %refs_3_.1, f32[4,2,128,128]{3,2,1,0:T(8,128)} %refs_3_.1), custom_call_target="tpu_custom_call" | custom-call | tf_op jit(solution)/shard_map/pallas_call | solution.py:170
  3.3 14.8 %all_to_all.5 = f32[128,2,128]{2,1,0:T(2,128)S(1)} all-to-all(f32[128,2,128]{2,1,0:T(2,128)S(1)} %bitcast.13), channel_id=1, replica_groups=mesh['node'=4,'dev'=8] {'node','dev'}, dimensions={0} | all-to-all | bytes 262144 | tf_op jit(solution)/shard_map/all_to_all | solution.py:151
  18.2 1.0 %shard_map.38 = f32[256,128]{1,0:T(8,128)} custom-call(f32[256,128]{1,0:T(8,128)S(1)} %bitcast.12, f32[256,128]{1,0:T(8,128)S(1)} %get-tuple-element.8.m_ref), custom_call_target="tpu_custom_call" | custom-call | tf_op jit(solution)/shard_map/pallas_call | solution.py:184

commit v10 on v9

--- a/solution.py
+++ b/solution.py
@@ -13,8 +13,11 @@
     return jnp.dot(a, b, precision=HI, preferred_element_type=F32)
 
 
-def mm_t(a, b):
-    return lax.dot_general(a, b, (((1,), (1,)), ((), ())), precision=HI, preferred_element_type=F32)
+def mm_t(a, b, precision=HI):
+    return lax.dot_general(a, b, (((1,), (1,)), ((), ())), precision=precision, preferred_element_type=F32)
+
+
+PICK = lax.Precision.HIGH
 
 
 def flip_bit(x, index, u, axis):
@@ -96,7 +99,7 @@
     x = jnp.concatenate(
         [s_ref[pl.ds(0, width, stride=2), :], s_ref[pl.ds(1, width, stride=2), :]], axis=0
     )
-    x = mm_t(x, b_t)
+    x = mm_t(x, b_t, PICK)
     rows2 = lax.broadcasted_iota(jnp.int32, (2 * width, width), 0)
     cols2 = lax.broadcasted_iota(jnp.int32, (2 * width, width), 1)
     for u in range(gbits):
@@ -105,7 +108,7 @@
         x = jnp.where(differ & row_cross[u], flipped, x)
     x_ref[...] = x
     x = x_ref[...]
-    h0 = mm_t(d, jnp.concatenate([g_ref[0, 0], g_ref[0, 1]], axis=0))
+    h0 = mm_t(d, jnp.concatenate([g_ref[0, 0], g_ref[0, 1]], axis=0), PICK)
     h0r = h0[:, :width]
     h0i = h0[:, width:]
     u_ri = mm(jnp.concatenate([x[:width], x[width:]], axis=1), jnp.concatenate(
@@ -114,7 +117,7 @@
     g1_rows = []
     for p in range(2):
         g1_rows += [g_ref[1, p, pl.ds(start, size), :] for start, size in order]
-    g1 = mm_t(jnp.concatenate(g1_rows, axis=0), c_t)
+    g1 = mm_t(jnp.concatenate(g1_rows, axis=0), c_t, PICK)
     cols = lax.broadcasted_iota(jnp.int32, (width, width), 1)
     taken = jnp.zeros((width, width), jnp.int32)
     at = 0
@@ -123,7 +126,7 @@
         taken = jnp.where(inside, cols - at + start, taken)
         at += size
     arrive = (rows == taken).astype(F32)
-    g2 = mm(jnp.concatenate([h_ref[0, 0], h_ref[0, 1]], axis=0), arrive)
+    g2 = jnp.dot(jnp.concatenate([h_ref[0, 0], h_ref[0, 1]], axis=0), arrive, precision=PICK, preferred_element_type=F32)
     m_ref[...] = mm(complex_block(h_ref[1, 0], h_ref[1, 1]), g2)
     y = mm(complex_block(g1[:width], g1[width:]), jnp.concatenate([u_ri[:, :width], u_ri[:, width:]], axis=0))
     y_ref[pl.ds(0, width, stride=2), :] = y[:width]

time: 19.3 us -> 19 us (0.984)
  Pallas kernels: 4.33 us -> 4.02 us
    pallas_call x1, Pallas kernels: 3.3 us -> 2.97 us  [local(): pl.pallas_call(lambda *refs: first_kernel(*refs, gbits=gbits, order=order...]
where the time goes in v10:
time: 19 us; the launch traced here: 18.9 us
  blocking collectives  14.8 us (78%)
  Pallas kernels  4.02 us (21%)
    all_to_all x1, blocking collectives, exchange(): return lax.all_to_all(y, ('node', 'dev'), 0, 0, tiled=True)  14.8 us
    pallas_call x1, Pallas kernels, local(): pl.pallas_call(lambda *refs: first_kernel(*refs, gbits=gbits, order=order...  2.97 us
    pallas_call x1, Pallas kernels, local(): pl.pallas_call(second_kernel, out_shape=jax.ShapeDtypeStruct((2 * width,...  1.04 us

profile of v10, /device:TPU:0, one launch (start us, length us, event | category | flops | bytes accessed | tf_op | source)
XLA Modules:
  0.0 18.9 jit_solution(451311770842338533)
XLA Ops:
  0.0 3.0 %shard_map.37 = (f32[256,128]{1,0:T(8,128)S(1)}, f32[256,128]{1,0:T(8,128)S(1)}) custom-call(s32[14]{0:T(128)} %refs_0_.1, f32[256,128]{1,0:T(8,128)} %bitcast.14, f32[4,2,128,128]{3,2,1,0:T(8,128)} %refs_3_.1, f32[4,2,128,128]{3,2,1,0:T(8,128)} %refs_3_.1), custom_call_target="tpu_custom_call" | custom-call | tf_op jit(solution)/shard_map/pallas_call | solution.py:173
  3.0 14.8 %all_to_all.5 = f32[128,2,128]{2,1,0:T(2,128)S(1)} all-to-all(f32[128,2,128]{2,1,0:T(2,128)S(1)} %bitcast.13), channel_id=1, replica_groups=mesh['node'=4,'dev'=8] {'node','dev'}, dimensions={0} | all-to-all | bytes 262144 | tf_op jit(solution)/shard_map/all_to_all | solution.py:154
  17.8 1.0 %shard_map.38 = f32[256,128]{1,0:T(8,128)} custom-call(f32[256,128]{1,0:T(8,128)S(1)} %bitcast.12, f32[256,128]{1,0:T(8,128)S(1)} %get-tuple-element.8.m_ref), custom_call_target="tpu_custom_call" | custom-call | tf_op jit(solution)/shard_map/pallas_call | solution.py:187

commit v11 on v10

--- a/solution.py
+++ b/solution.py
@@ -37,6 +37,16 @@
 
 def first_kernel(q_ref, s_ref, g_ref, h_ref, y_ref, m_ref, x_ref, pair_ref, *, gbits, order):
     width = 2**gbits
+    cols = lax.broadcasted_iota(jnp.int32, (width, width), 1)
+    taken = jnp.zeros((width, width), jnp.int32)
+    at = 0
+    for start, size in order:
+        inside = (cols >= at) & (cols < at + size)
+        taken = jnp.where(inside, cols - at + start, taken)
+        at += size
+    arrive = (lax.broadcasted_iota(jnp.int32, (width, width), 0) == taken).astype(F32)
+    g2 = jnp.dot(jnp.concatenate([h_ref[0, 0], h_ref[0, 1]], axis=0), arrive, precision=PICK, preferred_element_type=F32)
+    m_ref[...] = mm(complex_block(h_ref[1, 0], h_ref[1, 1]), g2)
     q = [q_ref[j] for j in range(2 * gbits)]
     for slot in range(2 * (gbits + 1)):
         pair_ref[slot] = gbits
@@ -118,16 +128,6 @@
     for p in range(2):
         g1_rows += [g_ref[1, p, pl.ds(start, size), :] for start, size in order]
     g1 = mm_t(jnp.concatenate(g1_rows, axis=0), c_t, PICK)
-    cols = lax.broadcasted_iota(jnp.int32, (width, width), 1)
-    taken = jnp.zeros((width, width), jnp.int32)
-    at = 0
-    for start, size in order:
-        inside = (cols >= at) & (cols < at + size)
-        taken = jnp.where(inside, cols - at + start, taken)
-        at += size
-    arrive = (rows == taken).astype(F32)
-    g2 = jnp.dot(jnp.concatenate([h_ref[0, 0], h_ref[0, 1]], axis=0), arrive, precision=PICK, preferred_element_type=F32)
-    m_ref[...] = mm(complex_block(h_ref[1, 0], h_ref[1, 1]), g2)
     y = mm(complex_block(g1[:width], g1[width:]), jnp.concatenate([u_ri[:, :width], u_ri[:, width:]], axis=0))
     y_ref[pl.ds(0, width, stride=2), :] = y[:width]
     y_ref[pl.ds(1, width, stride=2), :] = y[width:]

time: 19 us -> 18.9 us (level)
  no operation moved by 1% of the time
where the time goes in v11:
time: 18.9 us; the launch traced here: 18.7 us
  blocking collectives  14.8 us (78%)
  Pallas kernels  3.86 us (20%)
    all_to_all x1, blocking collectives, exchange(): return lax.all_to_all(y, ('node', 'dev'), 0, 0, tiled=True)  14.8 us
    pallas_call x1, Pallas kernels, local(): pl.pallas_call(lambda *refs: first_kernel(*refs, gbits=gbits, order=order...  2.83 us
    pallas_call x1, Pallas kernels, local(): pl.pallas_call(second_kernel, out_shape=jax.ShapeDtypeStruct((2 * width,...  1.03 us

profile of v11, /device:TPU:0, one launch (start us, length us, event | category | flops | bytes accessed | tf_op | source)
XLA Modules:
  0.0 18.7 jit_solution(3351422042533380485)
XLA Ops:
  0.0 2.8 %shard_map.37 = (f32[256,128]{1,0:T(8,128)S(1)}, f32[256,128]{1,0:T(8,128)S(1)}) custom-call(s32[14]{0:T(128)} %refs_0_.1, f32[256,128]{1,0:T(8,128)} %bitcast.14, f32[4,2,128,128]{3,2,1,0:T(8,128)} %refs_3_.1, f32[4,2,128,128]{3,2,1,0:T(8,128)} %refs_3_.1), custom_call_target="tpu_custom_call" | custom-call | tf_op jit(solution)/shard_map/pallas_call | solution.py:173
  2.8 14.8 %all_to_all.5 = f32[128,2,128]{2,1,0:T(2,128)S(1)} all-to-all(f32[128,2,128]{2,1,0:T(2,128)S(1)} %bitcast.13), channel_id=1, replica_groups=mesh['node'=4,'dev'=8] {'node','dev'}, dimensions={0} | all-to-all | bytes 262144 | tf_op jit(solution)/shard_map/all_to_all | solution.py:154
  17.7 1.0 %shard_map.38 = f32[256,128]{1,0:T(8,128)} custom-call(f32[256,128]{1,0:T(8,128)S(1)} %bitcast.12, f32[256,128]{1,0:T(8,128)S(1)} %get-tuple-element.8.m_ref), custom_call_target="tpu_custom_call" | custom-call | tf_op jit(solution)/shard_map/pallas_call | solution.py:187

commit v12 on v11

--- a/solution.py
+++ b/solution.py
@@ -61,39 +61,35 @@
         rank_row = rank_row + jnp.where(row_cross, 1, 0)
     row_of = [pair_ref[i] for i in range(gbits)]
     col_of = [pair_ref[gbits + 1 + i] for i in range(gbits)]
-    partner = [gbits] * gbits
-    partner_back = [gbits] * gbits
+    pt, bk, kp, cp = 2 * (gbits + 1), 3 * (gbits + 1), 4 * (gbits + 1), 5 * (gbits + 1)
+    for u in range(gbits):
+        pair_ref[pt + u] = gbits
+        pair_ref[bk + u] = gbits
     for i in range(gbits):
-        for a in range(gbits):
-            partner[a] = jnp.where(row_of[i] == a, col_of[i], partner[a])
-            partner_back[a] = jnp.where(col_of[i] == a, row_of[i], partner_back[a])
+        pair_ref[pt + row_of[i]] = col_of[i]
+        pair_ref[bk + col_of[i]] = row_of[i]
+    partner = [pair_ref[pt + u] for u in range(gbits)]
+    partner_back = [pair_ref[bk + u] for u in range(gbits)]
     row_cross = [partner[u] < gbits for u in range(gbits)]
     col_cross = [partner_back[u] < gbits for u in range(gbits)]
     held_at = 0
     for u in range(gbits):
-        pair_ref[jnp.where(row_cross[u], gbits, held_at)] = u
+        pair_ref[kp + jnp.where(row_cross[u], gbits, held_at)] = u
         held_at = held_at + jnp.where(row_cross[u], 0, 1)
-    kept = [pair_ref[u] for u in range(gbits)]
     col_pos = []
     stay_rank = 0
     for u in range(gbits):
-        free = kept[0]
-        for r in range(1, gbits):
-            free = jnp.where(stay_rank == r, kept[r], free)
+        free = pair_ref[kp + jnp.minimum(stay_rank, gbits)]
         col_pos.append(jnp.where(col_cross[u], partner_back[u], free))
+        pair_ref[cp + u] = col_pos[u]
         stay_rank = stay_rank + jnp.where(col_cross[u], 0, 1)
     pos = []
     for j in range(2 * gbits):
+        low = jnp.where(q[j] < gbits, q[j], 0)
         if j < gbits:
-            src_col = col_pos[0]
-            for u in range(1, gbits):
-                src_col = jnp.where(q[j] == u, col_pos[u], src_col)
-            pos.append(jnp.where(q[j] >= gbits, q[j] - gbits, src_col))
+            pos.append(jnp.where(q[j] >= gbits, q[j] - gbits, pair_ref[cp + low]))
         else:
-            back = partner_back[0]
-            for u in range(1, gbits):
-                back = jnp.where(q[j] == u, partner_back[u], back)
-            pos.append(jnp.where(q[j] < gbits, back, q[j] - gbits))
+            pos.append(jnp.where(q[j] < gbits, pair_ref[bk + low], q[j] - gbits))
     lane = lax.broadcasted_iota(jnp.int32, (1, width), 1)
     col_to = jnp.zeros((1, width), jnp.int32)
     row_from = jnp.zeros((1, width), jnp.int32)
@@ -181,7 +177,7 @@
             pl.BlockSpec((2, 2, width, width), lambda i: (1, 0, 0, 0)),
         ],
         out_specs=(vmem, vmem),
-        scratch_shapes=[pltpu.VMEM((2 * width, width), F32), pltpu.SMEM((2 * (gbits + 1),), jnp.int32)],
+        scratch_shapes=[pltpu.VMEM((2 * width, width), F32), pltpu.SMEM((6 * (gbits + 1),), jnp.int32)],
     )(qubit_order.astype(jnp.int32), rows, gates, gates)
     w = exchange(y.reshape(width, 2, width), width).reshape(2 * width, width)
     z = pl.pallas_call(

time: 18.9 us -> 18.8 us (level)
  no operation moved by 1% of the time
where the time goes in v12:
time: 18.8 us; the launch traced here: 18.6 us
  blocking collectives  14.8 us (79%)
  Pallas kernels  3.78 us (20%)
    all_to_all x1, blocking collectives, exchange(): return lax.all_to_all(y, ('node', 'dev'), 0, 0, tiled=True)  14.8 us
    pallas_call x1, Pallas kernels, local(): pl.pallas_call(lambda *refs: first_kernel(*refs, gbits=gbits, order=order...  2.75 us
    pallas_call x1, Pallas kernels, local(): pl.pallas_call(second_kernel, out_shape=jax.ShapeDtypeStruct((2 * width,...  1.03 us

profile of v12, /device:TPU:0, one launch (start us, length us, event | category | flops | bytes accessed | tf_op | source)
XLA Modules:
  0.0 18.6 jit_solution(18432680155065062568)
XLA Ops:
  0.0 2.7 %shard_map.37 = (f32[256,128]{1,0:T(8,128)S(1)}, f32[256,128]{1,0:T(8,128)S(1)}) custom-call(s32[14]{0:T(128)} %refs_0_.1, f32[256,128]{1,0:T(8,128)} %bitcast.14, f32[4,2,128,128]{3,2,1,0:T(8,128)} %refs_3_.1, f32[4,2,128,128]{3,2,1,0:T(8,128)} %refs_3_.1), custom_call_target="tpu_custom_call" | custom-call | tf_op jit(solution)/shard_map/pallas_call | solution.py:169
  2.8 14.8 %all_to_all.5 = f32[128,2,128]{2,1,0:T(2,128)S(1)} all-to-all(f32[128,2,128]{2,1,0:T(2,128)S(1)} %bitcast.13), channel_id=1, replica_groups=mesh['node'=4,'dev'=8] {'node','dev'}, dimensions={0} | all-to-all | bytes 262144 | tf_op jit(solution)/shard_map/all_to_all | solution.py:150
  17.6 1.0 %shard_map.38 = f32[256,128]{1,0:T(8,128)} custom-call(f32[256,128]{1,0:T(8,128)S(1)} %bitcast.12, f32[256,128]{1,0:T(8,128)S(1)} %get-tuple-element.8.m_ref), custom_call_target="tpu_custom_call" | custom-call | tf_op jit(solution)/shard_map/pallas_call | solution.py:183

commit v13 on v12

--- a/solution.py
+++ b/solution.py
@@ -112,8 +112,6 @@
         flipped = flip_bit(flip_bit(x, rows2, u, 0), cols2, u, 1)
         differ = (jnp.right_shift(rows2 ^ cols2, u) & 1) == 1
         x = jnp.where(differ & row_cross[u], flipped, x)
-    x_ref[...] = x
-    x = x_ref[...]
     h0 = mm_t(d, jnp.concatenate([g_ref[0, 0], g_ref[0, 1]], axis=0), PICK)
     h0r = h0[:, :width]
     h0i = h0[:, width:]

time: 18.8 us -> 18.8 us (level)
  no operation moved by 1% of the time
where the time goes in v13:
time: 18.8 us; the launch traced here: 18.6 us
  blocking collectives  14.8 us (79%)
  Pallas kernels  3.78 us (20%)
    all_to_all x1, blocking collectives, exchange(): return lax.all_to_all(y, ('node', 'dev'), 0, 0, tiled=True)  14.8 us
    pallas_call x1, Pallas kernels, local(): pl.pallas_call(lambda *refs: first_kernel(*refs, gbits=gbits, order=order...  2.75 us
    pallas_call x1, Pallas kernels, local(): pl.pallas_call(second_kernel, out_shape=jax.ShapeDtypeStruct((2 * width,...  1.03 us

profile of v13, /device:TPU:0, one launch (start us, length us, event | category | flops | bytes accessed | tf_op | source)
XLA Modules:
  0.0 18.6 jit_solution(18432680155065062568)
XLA Ops:
  0.0 2.7 %shard_map.37 = (f32[256,128]{1,0:T(8,128)S(1)}, f32[256,128]{1,0:T(8,128)S(1)}) custom-call(s32[14]{0:T(128)} %refs_0_.1, f32[256,128]{1,0:T(8,128)} %bitcast.14, f32[4,2,128,128]{3,2,1,0:T(8,128)} %refs_3_.1, f32[4,2,128,128]{3,2,1,0:T(8,128)} %refs_3_.1), custom_call_target="tpu_custom_call" | custom-call | tf_op jit(solution)/shard_map/pallas_call | solution.py:167
  2.8 14.8 %all_to_all.5 = f32[128,2,128]{2,1,0:T(2,128)S(1)} all-to-all(f32[128,2,128]{2,1,0:T(2,128)S(1)} %bitcast.13), channel_id=1, replica_groups=mesh['node'=4,'dev'=8] {'node','dev'}, dimensions={0} | all-to-all | bytes 262144 | tf_op jit(solution)/shard_map/all_to_all | solution.py:148
  17.6 1.0 %shard_map.38 = f32[256,128]{1,0:T(8,128)} custom-call(f32[256,128]{1,0:T(8,128)S(1)} %bitcast.12, f32[256,128]{1,0:T(8,128)S(1)} %get-tuple-element.8.m_ref), custom_call_target="tpu_custom_call" | custom-call | tf_op jit(solution)/shard_map/pallas_call | solution.py:181
